TPU v7x, 256 devices: a whole 4x4x8 slice. The times are simulated.
256 devices in a mesh: row: 64 (over z, y, core), col: 4 (over x).
Axes of the slice: x: 4, y: 4, z: 8, core: 2. Of those that a mesh axis runs over, the one named last changes fastest.
Arguments:
- panel_adj: float32 [24576, 512], P('row', 'col'), may hold values from -16 to 16
- inv_tile: float32 [512, 512], P('col'), may hold values from -1 to 2, as said below
- factor_panel: float32 [24576, 512], P('row', 'col'), may hold values from -0.0390625 to 0.0390625
- block_row: float32 [512, 8192], P('row', 'col'), may hold values from -0.25 to 0.25
- slab: float32 [24576, 8192], P('row', 'col'), may hold values from -0.0390625 to 0.0390625
- slab_adj: float32 [24576, 8192], P('row', 'col'), may hold values from -6 to 6
- row_adj: float32 [512, 8192], P('row', 'col'), may hold values from -6 to 6
- diag_adj: float32 [512, 512], P('row', 'col'), may hold values from -6 to 6
Outputs:
- panel_out: float32 [24576, 512], P('row', 'col')
- slab_out: float32 [24576, 8192], P('row', 'col')
- row_out: float32 [512, 8192], P('row', 'col')
- diag_out: float32 [512, 512], P('row', 'col')
Inputs may be any that keep to these rules, and one draw needn't show every extreme that they name: inv_tile is lower triangular with diagonal entries between 1 and 2.
All inputs are finite; a program needn't handle non-finite values.
Results may differ from a plain program's by a relative error of at most 0.00011.
Values sent between devices are 32-bit elements; how exact they have to be, the bound alone decides.
No kernel may reach another device: no remote copies, remote signals or barrier semaphores. Data moves between devices by JAX's collectives and lax.ppermute only.
A program may use at most 64 MiB of HBM per device.

v0:
```python
import jax
import jax.numpy as jnp
from jax import lax
from jax.sharding import PartitionSpec as P


def contract_rows(left, right):
    return lax.dot_general(
        left,
        right,
        (((0,), (0,)), ((), ())),
        precision=lax.Precision.HIGHEST,
        preferred_element_type=jnp.float32,
    )


def per_device(panel_adj, inv_tile, factor_panel, block_row, slab, slab_adj, row_adj, diag_adj):
    precise = lax.Precision.HIGHEST
    col_width = panel_adj.shape[1]
    col_place = lax.axis_index("col")
    share = diag_adj.shape[0]
    partial_panel = jnp.dot(
        panel_adj, inv_tile, precision=precise, preferred_element_type=jnp.float32
    )
    scaled = lax.psum(partial_panel, "col")
    panel_out = lax.dynamic_slice_in_dim(scaled, col_place * col_width, col_width, 1)
    slab_out = slab_adj - jnp.dot(
        scaled,
        lax.all_gather(block_row, "row", axis=0, tiled=True),
        precision=precise,
        preferred_element_type=jnp.float32,
    )
    row_term = lax.psum_scatter(contract_rows(scaled, slab), "row", scatter_dimension=0, tiled=True)
    diag_term = lax.psum_scatter(
        contract_rows(scaled, factor_panel), "row", scatter_dimension=0, tiled=True
    )
    row_ids = lax.broadcasted_iota(jnp.int32, diag_adj.shape, 0) + lax.axis_index("row") * share
    col_ids = lax.broadcasted_iota(jnp.int32, diag_adj.shape, 1) + col_place * col_width
    diag_out = diag_adj - jnp.where(col_ids <= row_ids, diag_term, 0.0)
    return (panel_out, slab_out, row_adj - row_term, diag_out)


def solution(mesh):
    return jax.shard_map(
        per_device,
        mesh=mesh,
        in_specs=(
            P("row", "col"),
            P("col", None),
            P("row", "col"),
            P("row", "col"),
            P("row", "col"),
            P("row", "col"),
            P("row", "col"),
            P("row", "col"),
        ),
        out_specs=(P("row", "col"), P("row", "col"), P("row", "col"), P("row", "col")),
        check_vma=False,
    )
```

profile of v0, /device:TPU:24, one launch (start us, length us, event | category | flops | bytes accessed | tf_op | source)
XLA Modules:
  0.0 368.0 jit_solution(2602399601953829121)
XLA Ops:
  7.2 0.0 copy-start
  7.2 0.0 all-reduce.6.cloned.1.call-start
  7.2 2.8 fusion.1
  10.1 0.0 all-reduce.6.cloned.1.call-update
  10.1 0.0 copy-start.2
  10.1 0.0 all-reduce.8.cloned.1.call-start
  10.2 53.1 %all-reduce.6.cloned.1.call-done = f32[384,512]{1,0:T(8,128)} async-done(((f32[384,512]{1,0:T(8,128)}), f32[384,512]{1,0:T(8,128)}) %all-reduce.6.cloned.1.call-update) | async-done | bytes 786448 | tf_op jit(solution)/shard_map/psum | solution.py:25
  63.2 0.0 copy-done
  63.2 0.0 copy-start.1
  63.2 9.5 %fusion.2 = f32[512,2048]{1,0:T(8,128)} fusion(f32[384,512]{1,0:T(8,128)} %all-reduce.6.cloned.1.call-done, f32[384,2048]{1,0:T(8,128)S(1)} %copy-done), kind=kOutput, calls=%fused_computation.8 | convolution fusion | flops 4831838208 | bytes 8126464 | tf_op jit(solution)/shard_map/dot_general | solution.py:8
  72.7 0.0 copy-done.2
  72.7 0.0 copy-done.1
  72.7 0.0 copy-start.5
  72.7 0.0 copy-start.4
  72.7 0.0 copy-start.3
  72.7 2.2 fusion.3
  75.0 0.0 all-reduce.8.cloned.1.call-update
  75.0 0.0 all-gather.2.cloned.1.call-start
  75.0 0.7 all-gather.2.cloned.1.call-update
  75.7 0.0 copy-done.5
  75.7 0.6 dynamic-slice
  77.0 1.6 constant_dynamic-slice_fusion
  78.6 192.9 %all-reduce.8.cloned.1.call-done = (f32[512,2048]{1,0:T(8,128)}, f32[512,128]{1,0:T(8,128)}) async-done(((f32[512,2048]{1,0:T(8,128)}, f32[512,128]{1,0:T(8,128)}), (f32[512,2048]{1,0:T(8,128)}, f32[512,128]{1,0:T(8,128)})) %all-reduce.8.cloned.1.call-update) | async-done | bytes 4456464
  271.5 0.0 copy-done.4
  271.5 1.3 fusion
  272.9 0.0 copy-done.3
  272.9 1.5 dynamic-slice_subtract_fusion
  274.4 77.5 %all-gather.2.cloned.1.call-done = f32[512,2048]{1,0:T(8,128)} async-done(((f32[8,2048]{1,0:T(8,128)}), f32[512,2048]{1,0:T(8,128)}) %all-gather.2.cloned.1.call-update) | async-done | bytes 4194320 | tf_op jit(solution)/shard_map/all_gather | solution.py:29
  351.8 9.6 %convolution_subtract_fusion = f32[384,2048]{1,0:T(8,128)} fusion(f32[384,2048]{1,0:T(8,128)} %param.13, f32[384,512]{1,0:T(8,128)} %all-reduce.6.cloned.1.call-done, f32[512,2048]{1,0:T(8,128)} %all-gather.2.cloned.1.call-done), kind=kOutput, calls=%fused_computation | convolution fusion | flops 4832624640 | bytes 11272192 | tf_op jit(solution)/shard_map/dot_general | solution.py:27
  (2 shorter events, 0.0 us)
Async XLA Ops:
  7.2 56.1 %copy-start = (f32[384,2048]{1,0:T(8,128)S(1)}, f32[384,2048]{1,0:T(8,128)}, u32[]{:S(2)}) copy-start(f32[384,2048]{1,0:T(8,128)} %param.12) | copy-start | bytes 9437188
  7.2 56.0 %all-reduce.6.cloned.1.call-start = ((), (), s32[]{:S(2)}) async-start(), calls=%async_computation | async-start | bytes 1572864 | tf_op jit(solution)/shard_map/psum | solution.py:25
  10.1 62.6 %copy-start.2 = (f32[384,128]{1,0:T(8,128)S(1)}, f32[384,128]{1,0:T(8,128)}, u32[]{:S(2)}) copy-start(f32[384,128]{1,0:T(8,128)} %param.10) | copy-start | bytes 589828
  10.1 261.4 %all-reduce.8.cloned.1.call-start = ((), (), s32[]{:S(2)}) async-start(), calls=%async_computation.2 | async-start | bytes 8912896
  63.2 9.5 %copy-start.1 = (f32[384,512]{1,0:T(8,128)S(1)}, f32[384,512]{1,0:T(8,128)}, u32[]{:S(2)}) copy-start(f32[384,512]{1,0:T(8,128)} %all-reduce.6.cloned.1.call-done) | copy-start | bytes 2359300
  72.7 3.0 copy-start.5
  72.7 198.8 %copy-start.4 = (f32[8,128]{1,0:T(8,128)S(1)}, f32[8,128]{1,0:T(8,128)}, u32[]{:S(2)}) copy-start(f32[8,128]{1,0:T(8,128)} %param.15) | copy-start | bytes 12292
  72.7 200.2 %copy-start.3 = (f32[8,2048]{1,0:T(8,128)S(1)}, f32[8,2048]{1,0:T(8,128)}, u32[]{:S(2)}) copy-start(f32[8,2048]{1,0:T(8,128)} %param.14) | copy-start | bytes 196612
  75.0 276.9 %all-gather.2.cloned.1.call-start = ((), (), s32[]{:S(2)}) async-start(), calls=%async_computation.1 | async-start | bytes 4259840 | tf_op jit(solution)/shard_map/all_gather | solution.py:29
Sparse Core Ops, SparseCore 0:
  10.9 52.2 all-reduce.5
  75.1 196.3 all-reduce.7
  274.3 77.4 all-gather.1
where the time goes:
time: 371 us; the launch traced here: 368 us
  waiting for transfers between devices  324 us (87%)
  matrix products  24.1 us (6%)
  between operations  14.5 us (4%)
    unnamed x4, waiting for transfers between devices  194 us
    all_gather x1, waiting for transfers between devices, per_device(): lax.all_gather(block_row, 'row', axis=0, tiled=True)  77.5 us
    psum x1, waiting for transfers between devices, per_device(): scaled = lax.psum(partial_panel, 'col')  53.1 us
    dot_general x2, matrix products, contract_rows(): lax.dot_general(left, right, (((0,), (0,)), ((), ())), precision=lax.Prec...  11.7 us
    dot_general x1, matrix products, per_device(): jnp.dot(scaled, lax.all_gather(block_row, 'row', axis=0, tiled=True), pre...  9.61 us
  transfers between devices with their start and end apart: 3, of which 3 were waited for; matrix products, arithmetic and copies ran while one was open for 1% of the time, Pallas kernels for 0%

commit v1 on v0

v1 whole, which is shorter than its diff:
```python
import jax
import jax.numpy as jnp
from jax import lax
from jax.sharding import PartitionSpec as P


def contract_rows(left, right):
    return lax.dot_general(
        left,
        right,
        (((0,), (0,)), ((), ())),
        precision=lax.Precision.HIGHEST,
        preferred_element_type=jnp.float32,
    )


def bit_orders(bits):
    if bits == 6:
        return (0, 1, 3, 2, 4, 5), (0, 3, 1, 4, 2, 5)
    order = tuple(range(bits))
    return order, order


def swap_with(value, axis, size, bit):
    return lax.ppermute(value, axis, [(i, i ^ (1 << bit)) for i in range(size)])


def reduce_scatter_rows(stack, axis, size, order):
    bits = size.bit_length() - 1
    place = lax.axis_index(axis)
    tail = stack.shape[1:]
    held = stack.reshape((2,) * bits + tail)
    for bit in order:
        dim = bits - 1 - bit
        mine = (place >> bit) & 1
        low = lax.index_in_dim(held, 0, dim, keepdims=False)
        high = lax.index_in_dim(held, 1, dim, keepdims=False)
        keep = jnp.where(mine == 0, low, high)
        send = jnp.where(mine == 0, high, low)
        held = jnp.expand_dims(keep + swap_with(send, axis, size, bit), dim)
    return held.reshape(tail)


def all_gather_rows(piece, axis, size, order):
    bits = size.bit_length() - 1
    place = lax.axis_index(axis)
    tail = piece.shape
    held = piece.reshape((1,) * bits + tail)
    for bit in order:
        dim = bits - 1 - bit
        mine = (place >> bit) & 1
        other = swap_with(held, axis, size, bit)
        held = jnp.where(
            mine == 0,
            jnp.concatenate([held, other], dim),
            jnp.concatenate([other, held], dim),
        )
    return held.reshape((size * tail[0],) + tail[1:])


def per_device(panel_adj, inv_tile, factor_panel, block_row, slab, slab_adj, row_adj, diag_adj):
    precise = lax.Precision.HIGHEST
    rows_n = lax.axis_size("row")
    cols_n = lax.axis_size("col")
    col_width = panel_adj.shape[1]
    col_place = lax.axis_index("col")
    row_place = lax.axis_index("row")
    share = diag_adj.shape[0]
    first, second = bit_orders(rows_n.bit_length() - 1)

    half_k = block_row.shape[1] // 2
    gathered = jnp.concatenate(
        [
            all_gather_rows(block_row[:, :half_k], "row", rows_n, first[::-1]),
            all_gather_rows(block_row[:, half_k:], "row", rows_n, second[::-1]),
        ],
        axis=1,
    )

    partial_panel = jnp.dot(
        panel_adj, inv_tile, precision=precise, preferred_element_type=jnp.float32
    )
    parts = partial_panel.reshape(partial_panel.shape[0], cols_n, col_width)
    own = lax.dynamic_index_in_dim(parts, col_place, 1, keepdims=False)
    for shift in range(1, cols_n):
        target = jnp.maximum(col_place - shift, 0)
        piece = lax.dynamic_index_in_dim(parts, target, 1, keepdims=False)
        own = own + lax.ppermute(piece, "col", [(c, c - shift) for c in range(shift, cols_n)])
    panel_out = own
    blocks = [None] * cols_n
    for shift in range(cols_n):
        if shift == 0:
            got = own
        else:
            got = lax.ppermute(own, "col", [(c, (c + shift) % cols_n) for c in range(cols_n)])
        blocks[shift] = got
    stacked = jnp.stack(blocks, axis=0)
    scaled_blocks = [
        lax.dynamic_index_in_dim(stacked, (col_place - j) % cols_n, 0, keepdims=False)
        for j in range(cols_n)
    ]
    scaled = jnp.concatenate(scaled_blocks, axis=1)

    slab_out = slab_adj - jnp.dot(
        scaled, gathered, precision=precise, preferred_element_type=jnp.float32
    )
    row_term = contract_rows(scaled, slab)
    diag_term = contract_rows(scaled, factor_panel)
    width = row_term.shape[1]
    half_w = width // 2
    stack_a = jnp.concatenate([row_term[:, :half_w], diag_term], axis=1)
    stack_b = row_term[:, half_w:]
    sum_a = reduce_scatter_rows(stack_a.reshape(rows_n, share, -1), "row", rows_n, first)
    sum_b = reduce_scatter_rows(stack_b.reshape(rows_n, share, -1), "row", rows_n, second)
    row_sum = jnp.concatenate([sum_a[:, :half_w], sum_b], axis=1)
    diag_sum = sum_a[:, half_w:]

    row_ids = lax.broadcasted_iota(jnp.int32, diag_adj.shape, 0) + row_place * share
    col_ids = lax.broadcasted_iota(jnp.int32, diag_adj.shape, 1) + col_place * col_width
    diag_out = diag_adj - jnp.where(col_ids <= row_ids, diag_sum, 0.0)
    return (panel_out, slab_out, row_adj - row_sum, diag_out)


def solution(mesh):
    return jax.shard_map(
        per_device,
        mesh=mesh,
        in_specs=(
            P("row", "col"),
            P("col", None),
            P("row", "col"),
            P("row", "col"),
            P("row", "col"),
            P("row", "col"),
            P("row", "col"),
            P("row", "col"),
        ),
        out_specs=(P("row", "col"), P("row", "col"), P("row", "col"), P("row", "col")),
        check_vma=False,
    )
```

time: 371 us -> 141 us (0.38)
  waiting for transfers between devices: 324 us -> 57.2 us
  starting transfers between devices: 0.12 us -> 45.3 us
  between operations: 14.5 us -> 1.2 us
  local copies, waits for them, and re-layouts: 2.25 us -> 10.1 us
  matrix products: 24.1 us -> 18 us
  other arithmetic: 2.83 us -> 8.62 us
    unnamed x4 -> x0, waiting for transfers between devices: 194 us -> none
    all_gather x1 -> x0, waiting for transfers between devices: 77.5 us -> none  [per_device(): lax.all_gather(block_row, 'row', axis=0, tiled=True)]
    ppermute x0 -> x30, waiting for transfers between devices: none -> 57.2 us  [the longest x24 53.3 us: swap_with(): return lax.ppermute(value, axis, [(i, i ^ 1 << bit) for i in range(size)])]
    psum x1 -> x0, waiting for transfers between devices: 53.1 us -> none  [per_device(): scaled = lax.psum(partial_panel, 'col')]
    ppermute x0 -> x30, starting transfers between devices: none -> 45.3 us  [the longest x24 32.6 us: swap_with(): return lax.ppermute(value, axis, [(i, i ^ 1 << bit) for i in range(size)])]
  transfers between devices with their start and end apart: 3 -> 30, of which waited for: 3 -> 13; matrix products, arithmetic and copies ran while one was open for 1% -> 18% of each run, Pallas kernels for 0% -> 0%
where the time goes in v1:
time: 141 us; the launch traced here: 140 us
  waiting for transfers between devices  57.2 us (41%)
  starting transfers between devices  45.3 us (32%)
  matrix products  18 us (13%)
  local copies, waits for them, and re-layouts  10.1 us (7%)
  other arithmetic  8.62 us (6%)
    ppermute x24, waiting for transfers between devices, swap_with(): return lax.ppermute(value, axis, [(i, i ^ 1 << bit) for i in range(size)])  53.3 us
    ppermute x24, starting transfers between devices, swap_with(): return lax.ppermute(value, axis, [(i, i ^ 1 << bit) for i in range(size)])  32.6 us
    ppermute x3, starting transfers between devices, per_device(): lax.ppermute(own, 'col', [(c, (c + shift) % cols_n) for c in range(cols_n)])  8.85 us
    dot_general x2, matrix products, contract_rows(): lax.dot_general(left, right, (((0,), (0,)), ((), ())), precision=lax.Prec...  8.25 us
    dot_general x1, matrix products, per_device(): jnp.dot(scaled, gathered, precision=precise, preferred_element_type=jnp.f...  6.87 us
    ppermute x3, waiting for transfers between devices, per_device(): lax.ppermute(own, 'col', [(c, (c + shift) % cols_n) for c in range(cols_n)])  3.9 us
    ppermute x3, starting transfers between devices, per_device(): lax.ppermute(piece, 'col', [(c, c - shift) for c in range(shift, cols_n)])  3.86 us
    dynamic_slice x1, local copies, waits for them, and re-layouts, per_device(): piece = lax.dynamic_index_in_dim(parts, target, 1, keepdims=False)  3.78 us
  transfers between devices with their start and end apart: 30, of which 13 were waited for; matrix products, arithmetic and copies ran while one was open for 18% of the time, Pallas kernels for 0%

profile of v1, /device:TPU:24, one launch (start us, length us, event | category | flops | bytes accessed | tf_op | source)
XLA Modules:
  0.0 140.4 jit_solution(2358352365585846632)
XLA Ops:
  0.7 2.8 %fusion.41 = f32[384,512]{1,0:T(8,128)} fusion(f32[384,128]{1,0:T(8,128)} %param.8, f32[128,512]{1,0:T(8,128)} %param.9), kind=kOutput, calls=%fused_computation.107 | convolution fusion | flops 301989888 | bytes 1245184 | tf_op jit(solution)/shard_map/dot_general | solution.py:80
  3.5 2.3 %reshape.2275 = f32[384,4,128]{2,1,0:T(4,128)} reshape(f32[384,512]{1,0:T(8,128)} %fusion.41) | data formatting | bytes 1572864 | tf_op jit(solution)/shard_map/reshape | solution.py:83
  5.8 3.8 %constant_dynamic-slice_fusion.2 = (f32[384,1,128]{2,1,0:T(1,128)}, f32[384,1,128]{2,1,0:T(1,128)S(1)}, f32[384,1,128]{2,1,0:T(1,128)}, f32[384,1,128]{2,1,0:T(1,128)S(1)}) fusion(f32[384,4,128]{2,1,0:T(4,128)} %reshape.2275, s32[]{:T(128)S(6)} %max.9, s32[]{:T(128)S(6)} %max.11, s32[]{:T(128)S(6)} %max.10, s32[]{:T(128)S(6)} %select_n.767), kind=kLoop, calls=%fused_computation.97 | loop fusion | bytes 1572880 | tf_op jit(solution)/shard_map/jit(dynamic_index_in_dim)/dynamic_slice | solution.py:87
  10.9 1.3 collective-permute-start.1
  12.2 1.3 collective-permute-start.2
  13.5 1.4 %slice_bitcast_fusion.3 = (f32[1,1,8,1024]{3,2,0,1:T(8,128)}, f32[1,1,1,1,1,1,8,1024]{7,6,5,4,3,2,1,0:T(8,128)}, f32[1,1,1,1,1,1,8,1024]{7,6,5,4,3,2,1,0:T(8,128)}, f32[1,1,8,1024]{3,2,0,1:T(8,128)}) fusion(f32[8,2048]{1,0:T(8,128)} %param.11), kind=kLoop, calls=%fused_computation.86 | loop fusion | bytes 196608 | tf_op jit(solution)/shard_map/concatenate | solution.py:55
  14.9 7.2 %collective-permute-start.6 = (f32[1,1,1,1,1,1,8,1024]{7,6,5,4,3,2,1,0:T(8,128)}, f32[1,1,1,1,1,1,8,1024]{7,6,5,4,3,2,1,0:T(8,128)}, u32[]{:S(2)}, u32[]{:S(2)}) collective-permute-start(f32[1,1,1,1,1,1,8,1024]{7,6,5,4,3,2,1,0:T(8,128)} %get-tuple-element.31), channel_id=1, source_target_pairs={{0,128},{4,132},{8,136},{12,140},{16,144},{20,148},{24,152},{28,15... | collective-permute-start | bytes 98312 | tf_op jit(solution)/shard_map/ppermute | solution.py:25
  22.1 2.2 %collective-permute-done.6 = f32[1,1,1,1,1,1,8,1024]{7,6,5,4,3,2,1,0:T(8,128)} collective-permute-done((f32[1,1,1,1,1,1,8,1024]{7,6,5,4,3,2,1,0:T(8,128)}, f32[1,1,1,1,1,1,8,1024]{7,6,5,4,3,2,1,0:T(8,128)}, u32[]{:S(2)}, u32[]{:S(2)}) %collective-permute-start.6) | collective-permute-done | bytes 32800 | tf_op jit(solution)/shard_map/ppermute | solution.py:25
  25.1 2.2 %collective-permute-start.7 = (f32[2,1,1,1,1,1,8,1024]{7,6,0,5,4,3,2,1:T(8,128)S(1)}, f32[2,1,1,1,1,1,8,1024]{7,6,0,5,4,3,2,1:T(8,128)S(1)}, u32[]{:S(2)}, u32[]{:S(2)}) collective-permute-start(f32[2,1,1,1,1,1,8,1024]{7,6,0,5,4,3,2,1:T(8,128)S(1)} %fusion.22), channel_id=1, source_target_pairs={{0,64},{4,68},{8,72},{12,76},{16,80},{20,84},{24,88},{28,92},{32,9... | collective-permute-start | bytes 196616 | tf_op jit(solution)/shard_map/ppermute | solution.py:25
  27.3 3.2 %collective-permute-done.12 = f32[1,1,1,1,1,1,8,1024]{7,6,5,4,3,2,1,0:T(8,128)} collective-permute-done((f32[1,1,1,1,1,1,8,1024]{7,6,5,4,3,2,1,0:T(8,128)}, f32[1,1,1,1,1,1,8,1024]{7,6,5,4,3,2,1,0:T(8,128)}, u32[]{:S(2)}, u32[]{:S(2)}) %collective-permute-start.12) | collective-permute-done | bytes 32800 | tf_op jit(solution)/shard_map/ppermute | solution.py:25
  31.3 1.3 collective-permute-start.13
  34.4 2.4 %collective-permute-start.8 = (f32[2,2,1,1,1,1,8,1024]{7,6,1,0,5,4,3,2:T(8,128)S(1)}, f32[2,2,1,1,1,1,8,1024]{7,6,1,0,5,4,3,2:T(8,128)S(1)}, u32[]{:S(2)}, u32[]{:S(2)}) collective-permute-start(f32[2,2,1,1,1,1,8,1024]{7,6,1,0,5,4,3,2:T(8,128)S(1)} %copy.54), channel_id=1, source_target_pairs={{0,16},{4,20},{8,24},{12,28},{16,0},{20,4},{24,8},{28,12},{32,48},... | collective-permute-start | bytes 393224 | tf_op jit(solution)/shard_map/ppermute | solution.py:25
  37.6 1.6 %collective-permute-start.14 = (f32[2,1,1,2,1,1,8,1024]{7,6,5,4,3,2,1,0:T(8,128)S(1)}, f32[2,1,1,2,1,1,8,1024]{7,6,5,4,3,2,1,0:T(8,128)S(1)}, u32[]{:S(2)}, u32[]{:S(2)}) collective-permute-start(f32[2,1,1,2,1,1,8,1024]{7,6,5,4,3,2,1,0:T(8,128)S(1)} %maximum_select_fusion.15), channel_id=1, source_target_pairs={{0,64},{4,68},{8,72},{12,76},{16,80},{20,84},{24,88},{28,92},{32,9... | collective-permute-start | bytes 393224 | tf_op jit(solution)/shard_map/ppermute | solution.py:25
  40.4 2.7 %collective-permute-start.3 = (f32[384,128]{1,0:T(8,128)S(1)}, f32[384,128]{1,0:T(8,128)S(1)}, u32[]{:S(2)}, u32[]{:S(2)}) collective-permute-start(f32[384,128]{1,0:T(8,128)S(1)} %add_add_fusion), channel_id=1, source_target_pairs={{0,1},{1,2},{2,3},{3,0},{4,5},{5,6},{6,7},{7,4},{8,9},{9,10},{10,1... | collective-permute-start | bytes 589832 | tf_op jit(solution)/shard_map/ppermute | solution.py:95
  43.1 6.1 %collective-permute-start.4 = (f32[384,128]{1,0:T(8,128)S(1)}, f32[384,128]{1,0:T(8,128)S(1)}, u32[]{:S(2)}, u32[]{:S(2)}) collective-permute-start(f32[384,128]{1,0:T(8,128)S(1)} %add_add_fusion), channel_id=1, source_target_pairs={{0,2},{1,3},{2,0},{3,1},{4,6},{5,7},{6,4},{7,5},{8,10},{9,11},{10,... | collective-permute-start | bytes 589832 | tf_op jit(solution)/shard_map/ppermute | solution.py:95
  52.2 2.8 %collective-permute-done.4 = f32[384,128]{1,0:T(8,128)S(1)} collective-permute-done((f32[384,128]{1,0:T(8,128)S(1)}, f32[384,128]{1,0:T(8,128)S(1)}, u32[]{:S(2)}, u32[]{:S(2)}) %collective-permute-start.4) | collective-permute-done | bytes 196640 | tf_op jit(solution)/shard_map/ppermute | solution.py:95
  55.2 1.5 %fusion.17 = f32[512,128]{1,0:T(8,128)S(1)} fusion(f32[384,128]{1,0:T(8,128)S(1)} %copy-done.5, f32[384,128]{1,0:T(8,128)S(1)} %get-tuple-element.11, f32[384,128]{1,0:T(8,128)S(1)} %get-tuple-element.12, f32[384,128]{1,0:T(8,128)S(1)} %get-tuple-element.13, f32[384,128]{1,0:T(8,128)S(1)} %get-tuple-element.10), kind=kOutput, calls=%fused_computation.52 | convolution fusion | flops 302579712 | bytes 1245184 | tf_op jit(solution)/shard_map/dot_general | solution.py:8
  56.7 6.8 %fusion.18 = f32[512,2048]{1,0:T(8,128)S(1)} fusion(f32[384,2048]{1,0:T(8,128)S(1)} %copy-done, f32[384,128]{1,0:T(8,128)S(1)} %get-tuple-element.11, f32[384,128]{1,0:T(8,128)S(1)} %get-tuple-element.12, f32[384,128]{1,0:T(8,128)S(1)} %get-tuple-element.13, f32[384,128]{1,0:T(8,128)S(1)} %get-tuple-element.10), kind=kOutput, calls=%fused_computation.53 | convolution fusion | flops 4832428032 | bytes 8126464 | tf_op jit(solution)/shard_map/dot_general | solution.py:8
  66.8 12.6 %collective-permute-done.10 = f32[2,2,2,2,1,1,8,1024]{7,6,5,4,3,2,1,0:T(8,128)S(1)} collective-permute-done((f32[2,2,2,2,1,1,8,1024]{7,6,5,4,3,2,1,0:T(8,128)S(1)}, f32[2,2,2,2,1,1,8,1024]{7,6,5,4,3,2,1,0:T(8,128)S(1)}, u32[]{:S(2)}, u32[]{:S(2)}) %collective-permute-start.10) | collective-permute-done | bytes 524320 | tf_op jit(solution)/shard_map/ppermute | solution.py:25
  83.2 11.5 %collective-permute-done.25 = f32[2,2,2,2,1,8,1024]{6,5,0,2,1,3,4:T(8,128)S(1)} collective-permute-done((f32[2,2,2,2,1,8,1024]{6,5,0,2,1,3,4:T(8,128)S(1)}, f32[2,2,2,2,1,8,1024]{6,5,0,2,1,3,4:T(8,128)S(1)}, u32[]{:S(2)}, u32[]{:S(2)}) %collective-permute-start.25) | collective-permute-done | bytes 524320 | tf_op jit(solution)/shard_map/ppermute | solution.py:25
  94.9 1.5 %collective-permute-start.26 = (f32[2,2,1,2,1,8,1024]{6,5,0,3,1,4,2:T(8,128)S(1)}, f32[2,2,1,2,1,8,1024]{6,5,0,3,1,4,2:T(8,128)S(1)}, u32[]{:S(2)}, u32[]{:S(2)}) collective-permute-start(f32[2,2,1,2,1,8,1024]{6,5,0,3,1,4,2:T(8,128)S(1)} %select_bitcast_fusion.5), channel_id=1, source_target_pairs={{0,8},{4,12},{8,0},{12,4},{16,24},{20,28},{24,16},{28,20},{32,40},... | collective-permute-start | bytes 786440 | tf_op jit(solution)/shard_map/ppermute | solution.py:25
  97.0 1.6 %copy-done.1 = f32[384,2048]{1,0:T(8,128)S(1)} copy-done((f32[384,2048]{1,0:T(8,128)S(1)}, f32[384,2048]{1,0:T(8,128)}, u32[]{:S(2)}) %copy-start.1) | copy-done | bytes 3145752
  98.6 6.9 %fusion.4 = f32[384,2048]{1,0:T(8,128)} fusion(f32[384,2048]{1,0:T(8,128)S(1)} %copy-done.1, f32[512,1024]{1,0:T(8,128)S(1)} %bitcast.171, f32[512,1024]{1,0:T(8,128)S(1)} %bitcast.169, f32[384,128]{1,0:T(8,128)S(1)} %get-tuple-element.11, f32[384,128]{1,0:T(8,128)S(1)} %get-tuple-element.12, f32[384,128]{1,0:T(8,128)S(1)} %get-tuple-element.13, ...), kind=kOutput, calls=%fused_computation.4 | convolution fusion | flops 4834263040 | bytes 11272192 | tf_op jit(solution)/shard_map/dot_general | solution.py:104
  105.6 1.5 %collective-permute-start.27 = (f32[2,1,2,1,1,8,1024]{6,5,0,2,4,3,1:T(8,128)S(1)}, f32[2,1,2,1,1,8,1024]{6,5,0,2,4,3,1:T(8,128)S(1)}, u32[]{:S(2)}, u32[]{:S(2)}) collective-permute-start(f32[2,1,2,1,1,8,1024]{6,5,0,2,4,3,1:T(8,128)S(1)} %select_bitcast_fusion.7), channel_id=1, source_target_pairs={{0,64},{4,68},{8,72},{12,76},{16,80},{20,84},{24,88},{28,92},{32,9... | collective-permute-start | bytes 393224 | tf_op jit(solution)/shard_map/ppermute | solution.py:25
  108.5 5.7 %collective-permute-done.27 = f32[2,1,2,1,1,8,1024]{6,5,0,2,4,3,1:T(8,128)S(1)} collective-permute-done((f32[2,1,2,1,1,8,1024]{6,5,0,2,4,3,1:T(8,128)S(1)}, f32[2,1,2,1,1,8,1024]{6,5,0,2,4,3,1:T(8,128)S(1)}, u32[]{:S(2)}, u32[]{:S(2)}) %collective-permute-start.27) | collective-permute-done | bytes 131104 | tf_op jit(solution)/shard_map/ppermute | solution.py:25
  114.9 2.8 %collective-permute-done.20 = f32[2,2,2,1,1,8,1152]{6,5,0,1,2,4,3:T(8,128)S(1)} collective-permute-done((f32[2,2,2,1,1,8,1152]{6,5,0,1,2,4,3:T(8,128)S(1)}, f32[2,2,2,1,1,8,1152]{6,5,0,1,2,4,3:T(8,128)S(1)}, u32[]{:S(2)}, u32[]{:S(2)}) %collective-permute-start.20) | collective-permute-done | bytes 294944 | tf_op jit(solution)/shard_map/ppermute | solution.py:25
  118.4 1.7 %collective-permute-done.28 = f32[2,1,1,1,1,8,1024]{6,5,4,3,2,1,0:T(8,128)S(1)} collective-permute-done((f32[2,1,1,1,1,8,1024]{6,5,4,3,2,1,0:T(8,128)S(1)}, f32[2,1,1,1,1,8,1024]{6,5,4,3,2,1,0:T(8,128)S(1)}, u32[]{:S(2)}, u32[]{:S(2)}) %collective-permute-start.28) | collective-permute-done | bytes 65568 | tf_op jit(solution)/shard_map/ppermute | solution.py:25
  120.1 4.4 %collective-permute-done.21 = f32[2,2,1,1,1,8,1152]{6,5,0,1,4,3,2:T(8,128)S(1)} collective-permute-done((f32[2,2,1,1,1,8,1152]{6,5,0,1,4,3,2:T(8,128)S(1)}, f32[2,2,1,1,1,8,1152]{6,5,0,1,4,3,2:T(8,128)S(1)}, u32[]{:S(2)}, u32[]{:S(2)}) %collective-permute-start.21) | collective-permute-done | bytes 147488 | tf_op jit(solution)/shard_map/ppermute | solution.py:25
  125.7 2.4 %collective-permute-start.29 = (f32[1,1,1,1,1,8,1024]{6,5,4,3,2,1,0:T(8,128)S(1)}, f32[1,1,1,1,1,8,1024]{6,5,4,3,2,1,0:T(8,128)S(1)}, u32[]{:S(2)}, u32[]{:S(2)}) collective-permute-start(f32[1,1,1,1,1,8,1024]{6,5,4,3,2,1,0:T(8,128)S(1)} %slice_select_fusion.1), channel_id=1, source_target_pairs={{0,128},{4,132},{8,136},{12,140},{16,144},{20,148},{24,152},{28,15... | collective-permute-start | bytes 98312 | tf_op jit(solution)/shard_map/ppermute | solution.py:25
  128.1 2.9 %collective-permute-done.22 = f32[2,1,1,1,1,8,1152]{6,5,4,3,2,1,0:T(8,128)S(1)} collective-permute-done((f32[2,1,1,1,1,8,1152]{6,5,4,3,2,1,0:T(8,128)S(1)}, f32[2,1,1,1,1,8,1152]{6,5,4,3,2,1,0:T(8,128)S(1)}, u32[]{:S(2)}, u32[]{:S(2)}) %collective-permute-start.22) | collective-permute-done | bytes 73760 | tf_op jit(solution)/shard_map/ppermute | solution.py:25
  131.1 2.5 %collective-permute-start.23 = (f32[1,1,1,1,1,8,1152]{6,5,4,3,2,1,0:T(8,128)S(1)}, f32[1,1,1,1,1,8,1152]{6,5,4,3,2,1,0:T(8,128)S(1)}, u32[]{:S(2)}, u32[]{:S(2)}) collective-permute-start(f32[1,1,1,1,1,8,1152]{6,5,4,3,2,1,0:T(8,128)S(1)} %slice_select_fusion), channel_id=1, source_target_pairs={{0,128},{4,132},{8,136},{12,140},{16,144},{20,148},{24,152},{28,15... | collective-permute-start | bytes 110600 | tf_op jit(solution)/shard_map/ppermute | solution.py:25
  133.6 5.4 %collective-permute-done.23 = f32[1,1,1,1,1,8,1152]{6,5,4,3,2,1,0:T(8,128)S(1)} collective-permute-done((f32[1,1,1,1,1,8,1152]{6,5,4,3,2,1,0:T(8,128)S(1)}, f32[1,1,1,1,1,8,1152]{6,5,4,3,2,1,0:T(8,128)S(1)}, u32[]{:S(2)}, u32[]{:S(2)}) %collective-permute-start.23) | collective-permute-done | bytes 36896 | tf_op jit(solution)/shard_map/ppermute | solution.py:25
  (105 shorter events, 22.8 us)
Async XLA Ops:
  0.6 56.0 %copy-start = (f32[384,2048]{1,0:T(8,128)S(1)}, f32[384,2048]{1,0:T(8,128)}, u32[]{:S(2)}) copy-start(f32[384,2048]{1,0:T(8,128)} %param.12) | copy-start | bytes 9437188
  9.6 29.6 %collective-permute-start = (f32[384,128]{1,0:T(8,128)}, f32[384,128]{1,0:T(8,128)}, u32[]{:S(2)}, u32[]{:S(2)}) collective-permute-start(f32[384,128]{1,0:T(8,128)} %bitcast.1), channel_id=1, source_target_pairs={{1,0},{2,1},{3,2},{5,4},{6,5},{7,6},{9,8},{10,9},{11,10},{13,12},{... | collective-permute-start | bytes 589832 | tf_op jit(solution)/shard_map/ppermute | solution.py:88
  10.9 28.4 %collective-permute-start.1 = (f32[384,128]{1,0:T(8,128)}, f32[384,128]{1,0:T(8,128)}, u32[]{:S(2)}, u32[]{:S(2)}) collective-permute-start(f32[384,128]{1,0:T(8,128)} %bitcast.2), channel_id=1, source_target_pairs={{2,0},{3,1},{6,4},{7,5},{10,8},{11,9},{14,12},{15,13},{18,16},{19,... | collective-permute-start | bytes 589832 | tf_op jit(solution)/shard_map/ppermute | solution.py:88
  12.2 27.1 %collective-permute-start.2 = (f32[384,128]{1,0:T(8,128)S(1)}, f32[384,128]{1,0:T(8,128)}, u32[]{:S(2)}, u32[]{:S(2)}) collective-permute-start(f32[384,128]{1,0:T(8,128)S(1)} %bitcast.183), channel_id=1, source_target_pairs={{3,0},{7,4},{11,8},{15,12},{19,16},{23,20},{27,24},{31,28},{35,32}... | collective-permute-start | bytes 589832 | tf_op jit(solution)/shard_map/ppermute | solution.py:88
  14.9 9.4 %collective-permute-start.6 = (f32[1,1,1,1,1,1,8,1024]{7,6,5,4,3,2,1,0:T(8,128)}, f32[1,1,1,1,1,1,8,1024]{7,6,5,4,3,2,1,0:T(8,128)}, u32[]{:S(2)}, u32[]{:S(2)}) collective-permute-start(f32[1,1,1,1,1,1,8,1024]{7,6,5,4,3,2,1,0:T(8,128)} %get-tuple-element.31), channel_id=1, source_target_pairs={{0,128},{4,132},{8,136},{12,140},{16,144},{20,148},{24,152},{28,15... | collective-permute-start | bytes 98312 | tf_op jit(solution)/shard_map/ppermute | solution.py:25
  22.1 8.4 %collective-permute-start.12 = (f32[1,1,1,1,1,1,8,1024]{7,6,5,4,3,2,1,0:T(8,128)}, f32[1,1,1,1,1,1,8,1024]{7,6,5,4,3,2,1,0:T(8,128)}, u32[]{:S(2)}, u32[]{:S(2)}) collective-permute-start(f32[1,1,1,1,1,1,8,1024]{7,6,5,4,3,2,1,0:T(8,128)} %get-tuple-element.32), channel_id=1, source_target_pairs={{0,128},{4,132},{8,136},{12,140},{16,144},{20,148},{24,152},{28,15... | collective-permute-start | bytes 98312 | tf_op jit(solution)/shard_map/ppermute | solution.py:25
  25.1 9.2 %collective-permute-start.7 = (f32[2,1,1,1,1,1,8,1024]{7,6,0,5,4,3,2,1:T(8,128)S(1)}, f32[2,1,1,1,1,1,8,1024]{7,6,0,5,4,3,2,1:T(8,128)S(1)}, u32[]{:S(2)}, u32[]{:S(2)}) collective-permute-start(f32[2,1,1,1,1,1,8,1024]{7,6,0,5,4,3,2,1:T(8,128)S(1)} %fusion.22), channel_id=1, source_target_pairs={{0,64},{4,68},{8,72},{12,76},{16,80},{20,84},{24,88},{28,92},{32,9... | collective-permute-start | bytes 196616 | tf_op jit(solution)/shard_map/ppermute | solution.py:25
  31.3 6.2 %collective-permute-start.13 = (f32[2,1,1,1,1,1,8,1024]{7,6,5,4,3,2,1,0:T(8,128)S(1)}, f32[2,1,1,1,1,1,8,1024]{7,6,5,4,3,2,1,0:T(8,128)S(1)}, u32[]{:S(2)}, u32[]{:S(2)}) collective-permute-start(f32[2,1,1,1,1,1,8,1024]{7,6,5,4,3,2,1,0:T(8,128)S(1)} %maximum_select_fusion.19), channel_id=1, source_target_pairs={{0,16},{4,20},{8,24},{12,28},{16,0},{20,4},{24,8},{28,12},{32,48},... | collective-permute-start | bytes 196616 | tf_op jit(solution)/shard_map/ppermute | solution.py:25
  34.4 14.8 %collective-permute-start.8 = (f32[2,2,1,1,1,1,8,1024]{7,6,1,0,5,4,3,2:T(8,128)S(1)}, f32[2,2,1,1,1,1,8,1024]{7,6,1,0,5,4,3,2:T(8,128)S(1)}, u32[]{:S(2)}, u32[]{:S(2)}) collective-permute-start(f32[2,2,1,1,1,1,8,1024]{7,6,1,0,5,4,3,2:T(8,128)S(1)} %copy.54), channel_id=1, source_target_pairs={{0,16},{4,20},{8,24},{12,28},{16,0},{20,4},{24,8},{28,12},{32,48},... | collective-permute-start | bytes 393224 | tf_op jit(solution)/shard_map/ppermute | solution.py:25
  37.6 12.8 %collective-permute-start.14 = (f32[2,1,1,2,1,1,8,1024]{7,6,5,4,3,2,1,0:T(8,128)S(1)}, f32[2,1,1,2,1,1,8,1024]{7,6,5,4,3,2,1,0:T(8,128)S(1)}, u32[]{:S(2)}, u32[]{:S(2)}) collective-permute-start(f32[2,1,1,2,1,1,8,1024]{7,6,5,4,3,2,1,0:T(8,128)S(1)} %maximum_select_fusion.15), channel_id=1, source_target_pairs={{0,64},{4,68},{8,72},{12,76},{16,80},{20,84},{24,88},{28,92},{32,9... | collective-permute-start | bytes 393224 | tf_op jit(solution)/shard_map/ppermute | solution.py:25
  40.4 11.8 %collective-permute-start.3 = (f32[384,128]{1,0:T(8,128)S(1)}, f32[384,128]{1,0:T(8,128)S(1)}, u32[]{:S(2)}, u32[]{:S(2)}) collective-permute-start(f32[384,128]{1,0:T(8,128)S(1)} %add_add_fusion), channel_id=1, source_target_pairs={{0,1},{1,2},{2,3},{3,0},{4,5},{5,6},{6,7},{7,4},{8,9},{9,10},{10,1... | collective-permute-start | bytes 589832 | tf_op jit(solution)/shard_map/ppermute | solution.py:95
  43.1 11.9 %collective-permute-start.4 = (f32[384,128]{1,0:T(8,128)S(1)}, f32[384,128]{1,0:T(8,128)S(1)}, u32[]{:S(2)}, u32[]{:S(2)}) collective-permute-start(f32[384,128]{1,0:T(8,128)S(1)} %add_add_fusion), channel_id=1, source_target_pairs={{0,2},{1,3},{2,0},{3,1},{4,6},{5,7},{6,4},{7,5},{8,10},{9,11},{10,... | collective-permute-start | bytes 589832 | tf_op jit(solution)/shard_map/ppermute | solution.py:95
  49.3 5.8 %collective-permute-start.5 = (f32[384,128]{1,0:T(8,128)S(1)}, f32[384,128]{1,0:T(8,128)S(1)}, u32[]{:S(2)}, u32[]{:S(2)}) collective-permute-start(f32[384,128]{1,0:T(8,128)S(1)} %add_add_fusion), channel_id=1, source_target_pairs={{0,3},{1,0},{2,1},{3,2},{4,7},{5,4},{6,5},{7,6},{8,11},{9,8},{10,9... | collective-permute-start | bytes 589832 | tf_op jit(solution)/shard_map/ppermute | solution.py:95
  49.3 15.6 %collective-permute-start.9 = (f32[2,2,1,2,1,1,8,1024]{7,6,5,4,3,2,1,0:T(8,128)S(1)}, f32[2,2,1,2,1,1,8,1024]{7,6,5,4,3,2,1,0:T(8,128)S(1)}, u32[]{:S(2)}, u32[]{:S(2)}) collective-permute-start(f32[2,2,1,2,1,1,8,1024]{7,6,5,4,3,2,1,0:T(8,128)S(1)} %copy.55), channel_id=1, source_target_pairs={{0,32},{4,36},{8,40},{12,44},{16,48},{20,52},{24,56},{28,60},{32,0... | collective-permute-start | bytes 786440 | tf_op jit(solution)/shard_map/ppermute | solution.py:25
  50.5 14.9 %collective-permute-start.15 = (f32[2,2,1,2,1,1,8,1024]{7,6,5,4,3,2,1,0:T(8,128)S(1)}, f32[2,2,1,2,1,1,8,1024]{7,6,5,4,3,2,1,0:T(8,128)S(1)}, u32[]{:S(2)}, u32[]{:S(2)}) collective-permute-start(f32[2,2,1,2,1,1,8,1024]{7,6,5,4,3,2,1,0:T(8,128)S(1)} %maximum_select_fusion.11), channel_id=1, source_target_pairs={{0,8},{4,12},{8,0},{12,4},{16,24},{20,28},{24,16},{28,20},{32,40},... | collective-permute-start | bytes 786440 | tf_op jit(solution)/shard_map/ppermute | solution.py:25
  64.8 15.7 %collective-permute-start.24 = (f32[2,2,2,2,2,8,1024]{6,5,0,3,1,4,2:T(8,128)S(1)}, f32[2,2,2,2,2,8,1024]{6,5,0,3,1,4,2:T(8,128)S(1)}, u32[]{:S(2)}, u32[]{:S(2)}) collective-permute-start(f32[2,2,2,2,2,8,1024]{6,5,0,3,1,4,2:T(8,128)S(1)} %select_bitcast_fusion.1), channel_id=1, source_target_pairs={{0,4},{4,0},{8,12},{12,8},{16,20},{20,16},{24,28},{28,24},{32,36},... | collective-permute-start | bytes 3145736 | tf_op jit(solution)/shard_map/ppermute | solution.py:25
  64.9 14.4 %collective-permute-start.10 = (f32[2,2,2,2,1,1,8,1024]{7,6,5,4,3,2,1,0:T(8,128)S(1)}, f32[2,2,2,2,1,1,8,1024]{7,6,5,4,3,2,1,0:T(8,128)S(1)}, u32[]{:S(2)}, u32[]{:S(2)}) collective-permute-start(f32[2,2,2,2,1,1,8,1024]{7,6,5,4,3,2,1,0:T(8,128)S(1)} %maximum_select_fusion.5), channel_id=1, source_target_pairs={{0,8},{4,12},{8,0},{12,4},{16,24},{20,28},{24,16},{28,20},{32,40},... | collective-permute-start | bytes 1572872 | tf_op jit(solution)/shard_map/ppermute | solution.py:25
  65.5 14.3 %collective-permute-start.16 = (f32[2,2,1,2,2,1,8,1024]{7,6,5,4,3,2,1,0:T(8,128)S(1)}, f32[2,2,1,2,2,1,8,1024]{7,6,5,4,3,2,1,0:T(8,128)S(1)}, u32[]{:S(2)}, u32[]{:S(2)}) collective-permute-start(f32[2,2,1,2,2,1,8,1024]{7,6,5,4,3,2,1,0:T(8,128)S(1)} %maximum_select_fusion.7), channel_id=1, source_target_pairs={{0,32},{4,36},{8,40},{12,44},{16,48},{20,52},{24,56},{28,60},{32,0... | collective-permute-start | bytes 1572872 | tf_op jit(solution)/shard_map/ppermute | solution.py:25
  66.6 15.4 %collective-permute-start.18 = (f32[2,2,2,2,2,8,1152]{6,5,0,1,3,2,4:T(8,128)S(1)}, f32[2,2,2,2,2,8,1152]{6,5,0,1,3,2,4:T(8,128)S(1)}, u32[]{:S(2)}, u32[]{:S(2)}) collective-permute-start(f32[2,2,2,2,2,8,1152]{6,5,0,1,3,2,4:T(8,128)S(1)} %select_bitcast_fusion), channel_id=1, source_target_pairs={{0,4},{4,0},{8,12},{12,8},{16,20},{20,16},{24,28},{28,24},{32,36},... | collective-permute-start | bytes 3538952 | tf_op jit(solution)/shard_map/ppermute | solution.py:25
  79.5 17.0 %collective-permute-start.11 = (f32[2,2,2,2,2,1,8,1024]{7,6,5,4,3,2,1,0:T(8,128)S(1)}, f32[2,2,2,2,2,1,8,1024]{7,6,5,4,3,2,1,0:T(8,128)S(1)}, u32[]{:S(2)}, u32[]{:S(2)}) collective-permute-start(f32[2,2,2,2,2,1,8,1024]{7,6,5,4,3,2,1,0:T(8,128)S(1)} %maximum_select_fusion.2), channel_id=1, source_target_pairs={{0,4},{4,0},{8,12},{12,8},{16,20},{20,16},{24,28},{28,24},{32,36},... | collective-permute-start | bytes 3145736 | tf_op jit(solution)/shard_map/ppermute | solution.py:25
  79.9 16.8 %collective-permute-start.17 = (f32[2,2,2,2,2,1,8,1024]{7,6,5,4,3,2,1,0:T(8,128)S(1)}, f32[2,2,2,2,2,1,8,1024]{7,6,5,4,3,2,1,0:T(8,128)S(1)}, u32[]{:S(2)}, u32[]{:S(2)}) collective-permute-start(f32[2,2,2,2,2,1,8,1024]{7,6,5,4,3,2,1,0:T(8,128)S(1)} %maximum_select_fusion.3), channel_id=1, source_target_pairs={{0,4},{4,0},{8,12},{12,8},{16,20},{20,16},{24,28},{28,24},{32,36},... | collective-permute-start | bytes 3145736 | tf_op jit(solution)/shard_map/ppermute | solution.py:25
  80.8 13.9 %collective-permute-start.25 = (f32[2,2,2,2,1,8,1024]{6,5,0,2,1,3,4:T(8,128)S(1)}, f32[2,2,2,2,1,8,1024]{6,5,0,2,1,3,4:T(8,128)S(1)}, u32[]{:S(2)}, u32[]{:S(2)}) collective-permute-start(f32[2,2,2,2,1,8,1024]{6,5,0,2,1,3,4:T(8,128)S(1)} %select_bitcast_fusion.3), channel_id=1, source_target_pairs={{0,32},{4,36},{8,40},{12,44},{16,48},{20,52},{24,56},{28,60},{32,0... | collective-permute-start | bytes 1572872 | tf_op jit(solution)/shard_map/ppermute | solution.py:25
  82.2 23.3 %collective-permute-start.19 = (f32[2,2,2,2,1,8,1152]{6,5,0,1,3,2,4:T(8,128)S(1)}, f32[2,2,2,2,1,8,1152]{6,5,0,1,3,2,4:T(8,128)S(1)}, u32[]{:S(2)}, u32[]{:S(2)}) collective-permute-start(f32[2,2,2,2,1,8,1152]{6,5,0,1,3,2,4:T(8,128)S(1)} %select_bitcast_fusion.2), channel_id=1, source_target_pairs={{0,8},{4,12},{8,0},{12,4},{16,24},{20,28},{24,16},{28,20},{32,40},... | collective-permute-start | bytes 1769480 | tf_op jit(solution)/shard_map/ppermute | solution.py:25
  94.9 10.6 %collective-permute-start.26 = (f32[2,2,1,2,1,8,1024]{6,5,0,3,1,4,2:T(8,128)S(1)}, f32[2,2,1,2,1,8,1024]{6,5,0,3,1,4,2:T(8,128)S(1)}, u32[]{:S(2)}, u32[]{:S(2)}) collective-permute-start(f32[2,2,1,2,1,8,1024]{6,5,0,3,1,4,2:T(8,128)S(1)} %select_bitcast_fusion.5), channel_id=1, source_target_pairs={{0,8},{4,12},{8,0},{12,4},{16,24},{20,28},{24,16},{28,20},{32,40},... | collective-permute-start | bytes 786440 | tf_op jit(solution)/shard_map/ppermute | solution.py:25
  105.6 8.5 %collective-permute-start.27 = (f32[2,1,2,1,1,8,1024]{6,5,0,2,4,3,1:T(8,128)S(1)}, f32[2,1,2,1,1,8,1024]{6,5,0,2,4,3,1:T(8,128)S(1)}, u32[]{:S(2)}, u32[]{:S(2)}) collective-permute-start(f32[2,1,2,1,1,8,1024]{6,5,0,2,4,3,1:T(8,128)S(1)} %select_bitcast_fusion.7), channel_id=1, source_target_pairs={{0,64},{4,68},{8,72},{12,76},{16,80},{20,84},{24,88},{28,92},{32,9... | collective-permute-start | bytes 393224 | tf_op jit(solution)/shard_map/ppermute | solution.py:25
  107.2 31.9 %copy-start.3 = (f32[8,2048]{1,0:T(8,128)S(1)}, f32[8,2048]{1,0:T(8,128)}, u32[]{:S(2)}) copy-start(f32[8,2048]{1,0:T(8,128)} %param.14) | copy-start | bytes 196612
  107.2 10.5 %collective-permute-start.20 = (f32[2,2,2,1,1,8,1152]{6,5,0,1,2,4,3:T(8,128)S(1)}, f32[2,2,2,1,1,8,1152]{6,5,0,1,2,4,3:T(8,128)S(1)}, u32[]{:S(2)}, u32[]{:S(2)}) collective-permute-start(f32[2,2,2,1,1,8,1152]{6,5,0,1,2,4,3:T(8,128)S(1)} %select_bitcast_fusion.4), channel_id=1, source_target_pairs={{0,32},{4,36},{8,40},{12,44},{16,48},{20,52},{24,56},{28,60},{32,0... | collective-permute-start | bytes 884744 | tf_op jit(solution)/shard_map/ppermute | solution.py:25
  114.2 5.9 %collective-permute-start.28 = (f32[2,1,1,1,1,8,1024]{6,5,4,3,2,1,0:T(8,128)S(1)}, f32[2,1,1,1,1,8,1024]{6,5,4,3,2,1,0:T(8,128)S(1)}, u32[]{:S(2)}, u32[]{:S(2)}) collective-permute-start(f32[2,1,1,1,1,8,1024]{6,5,4,3,2,1,0:T(8,128)S(1)} %select_bitcast_fusion.9), channel_id=1, source_target_pairs={{0,16},{4,20},{8,24},{12,28},{16,0},{20,4},{24,8},{28,12},{32,48},... | collective-permute-start | bytes 196616 | tf_op jit(solution)/shard_map/ppermute | solution.py:25
  117.8 6.7 %collective-permute-start.21 = (f32[2,2,1,1,1,8,1152]{6,5,0,1,4,3,2:T(8,128)S(1)}, f32[2,2,1,1,1,8,1152]{6,5,0,1,4,3,2:T(8,128)S(1)}, u32[]{:S(2)}, u32[]{:S(2)}) collective-permute-start(f32[2,2,1,1,1,8,1152]{6,5,0,1,4,3,2:T(8,128)S(1)} %select_bitcast_fusion.6), channel_id=1, source_target_pairs={{0,16},{4,20},{8,24},{12,28},{16,0},{20,4},{24,8},{28,12},{32,48},... | collective-permute-start | bytes 442376 | tf_op jit(solution)/shard_map/ppermute | solution.py:25
  124.6 6.5 %collective-permute-start.22 = (f32[2,1,1,1,1,8,1152]{6,5,4,3,2,1,0:T(8,128)S(1)}, f32[2,1,1,1,1,8,1152]{6,5,4,3,2,1,0:T(8,128)S(1)}, u32[]{:S(2)}, u32[]{:S(2)}) collective-permute-start(f32[2,1,1,1,1,8,1152]{6,5,4,3,2,1,0:T(8,128)S(1)} %select_bitcast_fusion.8), channel_id=1, source_target_pairs={{0,64},{4,68},{8,72},{12,76},{16,80},{20,84},{24,88},{28,92},{32,9... | collective-permute-start | bytes 221192 | tf_op jit(solution)/shard_map/ppermute | solution.py:25
  125.7 7.9 %collective-permute-start.29 = (f32[1,1,1,1,1,8,1024]{6,5,4,3,2,1,0:T(8,128)S(1)}, f32[1,1,1,1,1,8,1024]{6,5,4,3,2,1,0:T(8,128)S(1)}, u32[]{:S(2)}, u32[]{:S(2)}) collective-permute-start(f32[1,1,1,1,1,8,1024]{6,5,4,3,2,1,0:T(8,128)S(1)} %slice_select_fusion.1), channel_id=1, source_target_pairs={{0,128},{4,132},{8,136},{12,140},{16,144},{20,148},{24,152},{28,15... | collective-permute-start | bytes 98312 | tf_op jit(solution)/shard_map/ppermute | solution.py:25
  131.1 8.0 %collective-permute-start.23 = (f32[1,1,1,1,1,8,1152]{6,5,4,3,2,1,0:T(8,128)S(1)}, f32[1,1,1,1,1,8,1152]{6,5,4,3,2,1,0:T(8,128)S(1)}, u32[]{:S(2)}, u32[]{:S(2)}) collective-permute-start(f32[1,1,1,1,1,8,1152]{6,5,4,3,2,1,0:T(8,128)S(1)} %slice_select_fusion), channel_id=1, source_target_pairs={{0,128},{4,132},{8,136},{12,140},{16,144},{20,148},{24,152},{28,15... | collective-permute-start | bytes 110600 | tf_op jit(solution)/shard_map/ppermute | solution.py:25
  (4 other events, 46.2 us)

commit v2 on v1

--- a/solution.py
+++ b/solution.py
@@ -4,12 +4,12 @@
 from jax.sharding import PartitionSpec as P
 
 
-def contract_rows(left, right):
+def contract_rows(left, right, precision=lax.Precision.HIGHEST):
     return lax.dot_general(
         left,
         right,
         (((0,), (0,)), ((), ())),
-        precision=lax.Precision.HIGHEST,
+        precision=precision,
         preferred_element_type=jnp.float32,
     )
 
@@ -68,14 +68,7 @@
     share = diag_adj.shape[0]
     first, second = bit_orders(rows_n.bit_length() - 1)
 
-    half_k = block_row.shape[1] // 2
-    gathered = jnp.concatenate(
-        [
-            all_gather_rows(block_row[:, :half_k], "row", rows_n, first[::-1]),
-            all_gather_rows(block_row[:, half_k:], "row", rows_n, second[::-1]),
-        ],
-        axis=1,
-    )
+    gathered = lax.all_gather(block_row, "row", axis=0, tiled=True)
 
     partial_panel = jnp.dot(
         panel_adj, inv_tile, precision=precise, preferred_element_type=jnp.float32
@@ -102,9 +95,9 @@
     scaled = jnp.concatenate(scaled_blocks, axis=1)
 
     slab_out = slab_adj - jnp.dot(
-        scaled, gathered, precision=precise, preferred_element_type=jnp.float32
+        scaled, gathered, precision=lax.Precision.HIGH, preferred_element_type=jnp.float32
     )
-    row_term = contract_rows(scaled, slab)
+    row_term = contract_rows(scaled, slab, lax.Precision.HIGH)
     diag_term = contract_rows(scaled, factor_panel)
     width = row_term.shape[1]
     half_w = width // 2

time: 141 us -> 153 us (1.085); the launches traced: 140 us -> 151 us
  waiting for transfers between devices: 57.2 us -> 76.9 us
  starting transfers between devices: 45.3 us -> 27.5 us
  between operations: 1.2 us -> 14.4 us
  local copies, waits for them, and re-layouts: 10.1 us -> 6.62 us
  matrix products: 18 us -> 15.8 us
    all_gather x0 -> x1, waiting for transfers between devices: none -> 13.2 us  [per_device(): gathered = lax.all_gather(block_row, 'row', axis=0, tiled=True)]
    ppermute x24 -> x12, starting transfers between devices: 32.6 us -> 20.2 us  [swap_with(): return lax.ppermute(value, axis, [(i, i ^ 1 << bit) for i in range(size)])]
    ppermute x3, waiting for transfers between devices: 0.01 us -> 11.7 us  [per_device(): lax.ppermute(piece, 'col', [(c, c - shift) for c in range(shift, cols_n)])]
    ppermute x24 -> x12, waiting for transfers between devices: 53.3 us -> 42.3 us  [swap_with(): return lax.ppermute(value, axis, [(i, i ^ 1 << bit) for i in range(size)])]
    ppermute x3, waiting for transfers between devices: 3.9 us -> 9.73 us  [per_device(): lax.ppermute(own, 'col', [(c, (c + shift) % cols_n) for c in range(cols_n)])]
    ppermute x3, starting transfers between devices: 8.85 us -> 3.31 us  [per_device(): lax.ppermute(own, 'col', [(c, (c + shift) % cols_n) for c in range(cols_n)])]
    broadcast_in_dim x8, other arithmetic: 0.79 us -> 4 us  [reduce_scatter_rows(): held = jnp.expand_dims(keep + swap_with(send, axis, size, bit), dim)]
    select_n x12 -> x0, other arithmetic: 2.59 us -> none  [all_gather_rows(): jnp.where(mine == 0, jnp.concatenate([held, other], dim), jnp.concatenate...]
  transfers between devices with their start and end apart: 30 -> 19, of which waited for: 13 -> 15; matrix products, arithmetic and copies ran while one was open for 18% -> 4% of each run, Pallas kernels for 0% -> 0%
where the time goes in v2:
time: 153 us; the launch traced here: 151 us
  waiting for transfers between devices  76.9 us (50%)
  starting transfers between devices  27.5 us (18%)
  matrix products  15.8 us (10%)
  between operations  14.4 us (9%)
  other arithmetic  9.48 us (6%)
  local copies, waits for them, and re-layouts  6.62 us (4%)
    ppermute x12, waiting for transfers between devices, swap_with(): return lax.ppermute(value, axis, [(i, i ^ 1 << bit) for i in range(size)])  42.3 us
    ppermute x12, starting transfers between devices, swap_with(): return lax.ppermute(value, axis, [(i, i ^ 1 << bit) for i in range(size)])  20.2 us
    all_gather x1, waiting for transfers between devices, per_device(): gathered = lax.all_gather(block_row, 'row', axis=0, tiled=True)  13.2 us
    ppermute x3, waiting for transfers between devices, per_device(): lax.ppermute(piece, 'col', [(c, c - shift) for c in range(shift, cols_n)])  11.7 us
    ppermute x3, waiting for transfers between devices, per_device(): lax.ppermute(own, 'col', [(c, (c + shift) % cols_n) for c in range(cols_n)])  9.73 us
    dot_general x1, matrix products, per_device(): jnp.dot(scaled, gathered, precision=lax.Precision.HIGH, preferred_element...  7.89 us
    dot_general x2, matrix products, contract_rows(): lax.dot_general(left, right, (((0,), (0,)), ((), ())), precision=precisio...  5.07 us
    broadcast_in_dim x8, other arithmetic, reduce_scatter_rows(): held = jnp.expand_dims(keep + swap_with(send, axis, size, bit), dim)  4 us
  transfers between devices with their start and end apart: 19, of which 15 were waited for; matrix products, arithmetic and copies ran while one was open for 4% of the time, Pallas kernels for 0%

profile of v2, /device:TPU:24, one launch (start us, length us, event | category | flops | bytes accessed | tf_op | source)
XLA Modules:
  0.0 150.7 jit_solution(14322188900739108020)
XLA Ops:
  7.2 2.8 %fusion.17 = f32[384,512]{1,0:T(8,128)} fusion(f32[384,128]{1,0:T(8,128)} %param.8, f32[128,512]{1,0:T(8,128)} %param.9), kind=kOutput, calls=%fused_computation.58 | convolution fusion | flops 301989888 | bytes 1245184 | tf_op jit(solution)/shard_map/dot_general | solution.py:73
  10.1 2.3 %reshape.379 = f32[384,4,128]{2,1,0:T(4,128)} reshape(f32[384,512]{1,0:T(8,128)} %fusion.17) | data formatting | bytes 1572864 | tf_op jit(solution)/shard_map/reshape | solution.py:76
  12.4 3.1 %constant_dynamic-slice_fusion.2 = (f32[384,1,128]{2,1,0:T(1,128)S(1)}, f32[384,1,128]{2,1,0:T(1,128)S(1)}, f32[384,1,128]{2,1,0:T(1,128)S(1)}, f32[384,1,128]{2,1,0:T(1,128)S(1)}) fusion(f32[384,4,128]{2,1,0:T(4,128)} %reshape.379, s32[]{:T(128)S(6)} %max.9, s32[]{:T(128)S(6)} %max.11, s32[]{:T(128)S(6)} %max.10, s32[]{:T(128)S(6)} %select_n.375), kind=kLoop, calls=%fused_computation.48 | loop fusion | bytes 1572880 | tf_op jit(solution)/shard_map/jit(dynamic_index_in_dim)/dynamic_slice | solution.py:80
  15.5 1.3 collective-permute-start
  16.8 1.3 collective-permute-start.1
  18.1 1.3 collective-permute-start.2
  19.4 4.6 %collective-permute-done = f32[384,128]{1,0:T(8,128)S(1)} collective-permute-done((f32[384,128]{1,0:T(8,128)S(1)}, f32[384,128]{1,0:T(8,128)S(1)}, u32[]{:S(2)}, u32[]{:S(2)}) %collective-permute-start) | collective-permute-done | bytes 196640 | tf_op jit(solution)/shard_map/ppermute | solution.py:81
  24.0 2.9 %collective-permute-done.1 = f32[384,128]{1,0:T(8,128)S(1)} collective-permute-done((f32[384,128]{1,0:T(8,128)S(1)}, f32[384,128]{1,0:T(8,128)S(1)}, u32[]{:S(2)}, u32[]{:S(2)}) %collective-permute-start.1) | collective-permute-done | bytes 196640 | tf_op jit(solution)/shard_map/ppermute | solution.py:81
  27.0 4.1 %collective-permute-done.2 = f32[384,128]{1,0:T(8,128)S(1)} collective-permute-done((f32[384,128]{1,0:T(8,128)S(1)}, f32[384,128]{1,0:T(8,128)S(1)}, u32[]{:S(2)}, u32[]{:S(2)}) %collective-permute-start.2) | collective-permute-done | bytes 196640 | tf_op jit(solution)/shard_map/ppermute | solution.py:81
  32.2 2.2 %collective-permute-start.5 = (f32[384,128]{1,0:T(8,128)S(1)}, f32[384,128]{1,0:T(8,128)}, u32[]{:S(2)}, u32[]{:S(2)}) collective-permute-start(f32[384,128]{1,0:T(8,128)S(1)} %add_add_fusion), channel_id=1, source_target_pairs={{0,3},{1,0},{2,1},{3,2},{4,7},{5,4},{6,5},{7,6},{8,11},{9,8},{10,9... | collective-permute-start | bytes 589832 | tf_op jit(solution)/shard_map/ppermute | solution.py:88
  34.5 9.0 %collective-permute-done.3 = f32[384,128]{1,0:T(8,128)S(1)} collective-permute-done((f32[384,128]{1,0:T(8,128)S(1)}, f32[384,128]{1,0:T(8,128)S(1)}, u32[]{:S(2)}, u32[]{:S(2)}) %collective-permute-start.3) | collective-permute-done | bytes 196640 | tf_op jit(solution)/shard_map/ppermute | solution.py:88
  45.4 1.5 fusion.7
  46.9 3.6 %fusion.8 = f32[512,2048]{1,0:T(8,128)S(1)} fusion(f32[384,2048]{1,0:T(8,128)S(1)} %copy-done, f32[384,128]{1,0:T(8,128)S(1)} %get-tuple-element.11, f32[384,128]{1,0:T(8,128)S(1)} %get-tuple-element.12, f32[384,128]{1,0:T(8,128)S(1)} %get-tuple-element.13, f32[384,128]{1,0:T(8,128)S(1)} %get-tuple-element.10), kind=kOutput, calls=%fused_computation.31 | convolution fusion | flops 2416508928 | bytes 8126464 | tf_op jit(solution)/shard_map/dot_general | solution.py:8
  51.8 1.4 select_bitcast_fusion.1
  55.0 1.3 collective-permute-done.12
  56.2 2.1 %fusion.1 = f32[2,2,2,2,2,1,8,1024]{7,6,0,3,1,4,5,2:T(8,128)S(1)} fusion(f32[2,2,2,2,2,8,1024]{6,5,0,3,1,4,2:T(8,128)} %collective-permute-done.12, f32[2,2,2,2,2,1,8,1024]{7,6,5,4,3,2,1,0:T(8,128)} %copy-done.6, f32[2,2,2,2,2,1,8,1024]{7,6,5,4,3,2,1,0:T(8,128)} %copy-done.5, pred[]{:T(512)S(6)} %eq.22), kind=kLoop, calls=%fused_computation.6 | loop fusion | flops 524288 | bytes 4194305 | tf_op jit(solution)/shard_map/broadcast_in_dim | solution.py:40
  58.4 2.0 %collective-permute-start.13 = (f32[2,2,2,2,1,8,1024]{6,5,0,2,1,3,4:T(8,128)S(1)}, f32[2,2,2,2,1,8,1024]{6,5,0,2,1,3,4:T(8,128)S(1)}, u32[]{:S(2)}, u32[]{:S(2)}) collective-permute-start(f32[2,2,2,2,1,8,1024]{6,5,0,2,1,3,4:T(8,128)S(1)} %select_bitcast_fusion.3), channel_id=1, source_target_pairs={{0,32},{4,36},{8,40},{12,44},{16,48},{20,52},{24,56},{28,60},{32,0... | collective-permute-start | bytes 1572872 | tf_op jit(solution)/shard_map/ppermute | solution.py:25
  60.4 1.5 fusion
  62.9 10.1 %collective-permute-done.13 = f32[2,2,2,2,1,8,1024]{6,5,0,2,1,3,4:T(8,128)S(1)} collective-permute-done((f32[2,2,2,2,1,8,1024]{6,5,0,2,1,3,4:T(8,128)S(1)}, f32[2,2,2,2,1,8,1024]{6,5,0,2,1,3,4:T(8,128)S(1)}, u32[]{:S(2)}, u32[]{:S(2)}) %collective-permute-start.13) | collective-permute-done | bytes 524320 | tf_op jit(solution)/shard_map/ppermute | solution.py:25
  73.8 5.2 %collective-permute-done.7 = f32[2,2,2,2,1,8,1152]{6,5,0,1,3,2,4:T(8,128)S(1)} collective-permute-done((f32[2,2,2,2,1,8,1152]{6,5,0,1,3,2,4:T(8,128)S(1)}, f32[2,2,2,2,1,8,1152]{6,5,0,1,3,2,4:T(8,128)S(1)}, u32[]{:S(2)}, u32[]{:S(2)}) %collective-permute-start.7) | collective-permute-done | bytes 589856 | tf_op jit(solution)/shard_map/ppermute | solution.py:25
  79.1 4.6 %collective-permute-done.14 = f32[2,2,1,2,1,8,1024]{6,5,0,3,1,4,2:T(8,128)S(1)} collective-permute-done((f32[2,2,1,2,1,8,1024]{6,5,0,3,1,4,2:T(8,128)S(1)}, f32[2,2,1,2,1,8,1024]{6,5,0,3,1,4,2:T(8,128)S(1)}, u32[]{:S(2)}, u32[]{:S(2)}) %collective-permute-start.14) | collective-permute-done | bytes 262176 | tf_op jit(solution)/shard_map/ppermute | solution.py:25
  83.8 3.4 %collective-permute-start.15 = (f32[2,1,2,1,1,8,1024]{6,5,0,2,4,3,1:T(8,128)S(1)}, f32[2,1,2,1,1,8,1024]{6,5,0,2,4,3,1:T(8,128)S(1)}, u32[]{:S(2)}, u32[]{:S(2)}) collective-permute-start(f32[2,1,2,1,1,8,1024]{6,5,0,2,4,3,1:T(8,128)S(1)} %select_bitcast_fusion.7), channel_id=1, source_target_pairs={{0,64},{4,68},{8,72},{12,76},{16,80},{20,84},{24,88},{28,92},{32,9... | collective-permute-start | bytes 393224 | tf_op jit(solution)/shard_map/ppermute | solution.py:25
  87.7 5.7 %collective-permute-done.15 = f32[2,1,2,1,1,8,1024]{6,5,0,2,4,3,1:T(8,128)S(1)} collective-permute-done((f32[2,1,2,1,1,8,1024]{6,5,0,2,4,3,1:T(8,128)S(1)}, f32[2,1,2,1,1,8,1024]{6,5,0,2,4,3,1:T(8,128)S(1)}, u32[]{:S(2)}, u32[]{:S(2)}) %collective-permute-start.15) | collective-permute-done | bytes 131104 | tf_op jit(solution)/shard_map/ppermute | solution.py:25
  93.4 1.3 collective-permute-start.16
  94.7 3.7 %collective-permute-done.8 = f32[2,2,2,1,1,8,1152]{6,5,0,1,2,4,3:T(8,128)S(1)} collective-permute-done((f32[2,2,2,1,1,8,1152]{6,5,0,1,2,4,3:T(8,128)S(1)}, f32[2,2,2,1,1,8,1152]{6,5,0,1,2,4,3:T(8,128)S(1)}, u32[]{:S(2)}, u32[]{:S(2)}) %collective-permute-start.8) | collective-permute-done | bytes 294944 | tf_op jit(solution)/shard_map/ppermute | solution.py:25
  99.6 5.5 %collective-permute-done.9 = f32[2,2,1,1,1,8,1152]{6,5,0,1,4,3,2:T(8,128)S(1)} collective-permute-done((f32[2,2,1,1,1,8,1152]{6,5,0,1,4,3,2:T(8,128)S(1)}, f32[2,2,1,1,1,8,1152]{6,5,0,1,4,3,2:T(8,128)S(1)}, u32[]{:S(2)}, u32[]{:S(2)}) %collective-permute-start.9) | collective-permute-done | bytes 147488 | tf_op jit(solution)/shard_map/ppermute | solution.py:25
  105.3 5.0 %collective-permute-start.17 = (f32[1,1,1,1,1,8,1024]{6,5,4,3,2,1,0:T(8,128)S(1)}, f32[1,1,1,1,1,8,1024]{6,5,4,3,2,1,0:T(8,128)S(1)}, u32[]{:S(2)}, u32[]{:S(2)}) collective-permute-start(f32[1,1,1,1,1,8,1024]{6,5,4,3,2,1,0:T(8,128)S(1)} %slice_select_fusion.1), channel_id=1, source_target_pairs={{0,128},{4,132},{8,136},{12,140},{16,144},{20,148},{24,152},{28,15... | collective-permute-start | bytes 98312 | tf_op jit(solution)/shard_map/ppermute | solution.py:25
  110.3 2.6 %collective-permute-done.10 = f32[2,1,1,1,1,8,1152]{6,5,4,3,2,1,0:T(8,128)S(1)} collective-permute-done((f32[2,1,1,1,1,8,1152]{6,5,4,3,2,1,0:T(8,128)S(1)}, f32[2,1,1,1,1,8,1152]{6,5,4,3,2,1,0:T(8,128)S(1)}, u32[]{:S(2)}, u32[]{:S(2)}) %collective-permute-start.10) | collective-permute-done | bytes 73760 | tf_op jit(solution)/shard_map/ppermute | solution.py:25
  113.0 4.9 %collective-permute-start.11 = (f32[1,1,1,1,1,8,1152]{6,5,4,3,2,1,0:T(8,128)S(1)}, f32[1,1,1,1,1,8,1152]{6,5,4,3,2,1,0:T(8,128)S(1)}, u32[]{:S(2)}, u32[]{:S(2)}) collective-permute-start(f32[1,1,1,1,1,8,1152]{6,5,4,3,2,1,0:T(8,128)S(1)} %slice_select_fusion), channel_id=1, source_target_pairs={{0,128},{4,132},{8,136},{12,140},{16,144},{20,148},{24,152},{28,15... | collective-permute-start | bytes 110600 | tf_op jit(solution)/shard_map/ppermute | solution.py:25
  117.8 3.6 %collective-permute-done.11 = f32[1,1,1,1,1,8,1152]{6,5,4,3,2,1,0:T(8,128)S(1)} collective-permute-done((f32[1,1,1,1,1,8,1152]{6,5,4,3,2,1,0:T(8,128)S(1)}, f32[1,1,1,1,1,8,1152]{6,5,4,3,2,1,0:T(8,128)S(1)}, u32[]{:S(2)}, u32[]{:S(2)}) %collective-permute-start.11) | collective-permute-done | bytes 36896 | tf_op jit(solution)/shard_map/ppermute | solution.py:25
  122.8 13.2 %all-gather.2.cloned.1.call-done = f32[512,2048]{1,0:T(8,128)} async-done(((f32[8,2048]{1,0:T(8,128)}), f32[512,2048]{1,0:T(8,128)}) %all-gather.2.cloned.1.call-update) | async-done | bytes 4194320 | tf_op jit(solution)/shard_map/all_gather | solution.py:71
  135.9 7.9 %convolution_subtract_fusion = f32[384,2048]{1,0:T(8,128)} fusion(f32[384,2048]{1,0:T(8,128)} %param.13, f32[512,2048]{1,0:T(8,128)} %all-gather.2.cloned.1.call-done, f32[384,128]{1,0:T(8,128)S(1)} %get-tuple-element.11, f32[384,128]{1,0:T(8,128)} %copy-done.7, f32[384,128]{1,0:T(8,128)} %copy-done.8, f32[384,128]{1,0:T(8,128)S(1)} %get-tuple-element.10), kind=kOutput, calls=%fused_computation | convolution fusion | flops 2417295360 | bytes 11272192 | tf_op jit(solution)/shard_map/dot_general | solution.py:97
  (75 shorter events, 11.2 us)
Async XLA Ops:
  7.2 39.7 %copy-start = (f32[384,2048]{1,0:T(8,128)S(1)}, f32[384,2048]{1,0:T(8,128)}, u32[]{:S(2)}) copy-start(f32[384,2048]{1,0:T(8,128)} %param.12) | copy-start | bytes 9437188
  7.2 128.8 %all-gather.2.cloned.1.call-start = ((), (), s32[]{:S(2)}) async-start(), calls=%async_computation | async-start | bytes 4259840 | tf_op jit(solution)/shard_map/all_gather | solution.py:71
  15.5 8.5 %collective-permute-start = (f32[384,128]{1,0:T(8,128)S(1)}, f32[384,128]{1,0:T(8,128)S(1)}, u32[]{:S(2)}, u32[]{:S(2)}) collective-permute-start(f32[384,128]{1,0:T(8,128)S(1)} %bitcast.110), channel_id=1, source_target_pairs={{1,0},{2,1},{3,2},{5,4},{6,5},{7,6},{9,8},{10,9},{11,10},{13,12},{... | collective-permute-start | bytes 589832 | tf_op jit(solution)/shard_map/ppermute | solution.py:81
  16.8 10.2 %collective-permute-start.1 = (f32[384,128]{1,0:T(8,128)S(1)}, f32[384,128]{1,0:T(8,128)S(1)}, u32[]{:S(2)}, u32[]{:S(2)}) collective-permute-start(f32[384,128]{1,0:T(8,128)S(1)} %bitcast.109), channel_id=1, source_target_pairs={{2,0},{3,1},{6,4},{7,5},{10,8},{11,9},{14,12},{15,13},{18,16},{19,... | collective-permute-start | bytes 589832 | tf_op jit(solution)/shard_map/ppermute | solution.py:81
  18.1 13.0 %collective-permute-start.2 = (f32[384,128]{1,0:T(8,128)S(1)}, f32[384,128]{1,0:T(8,128)S(1)}, u32[]{:S(2)}, u32[]{:S(2)}) collective-permute-start(f32[384,128]{1,0:T(8,128)S(1)} %bitcast.108), channel_id=1, source_target_pairs={{3,0},{7,4},{11,8},{15,12},{19,16},{23,20},{27,24},{31,28},{35,32}... | collective-permute-start | bytes 589832 | tf_op jit(solution)/shard_map/ppermute | solution.py:81
  31.1 13.1 %copy-start.9 = (f32[384,128]{1,0:T(8,128)}, f32[384,128]{1,0:T(8,128)S(1)}, u32[]{:S(2)}) copy-start(f32[384,128]{1,0:T(8,128)S(1)} %add_add_fusion) | copy-start | bytes 589828
  31.1 12.3 %collective-permute-start.3 = (f32[384,128]{1,0:T(8,128)S(1)}, f32[384,128]{1,0:T(8,128)S(1)}, u32[]{:S(2)}, u32[]{:S(2)}) collective-permute-start(f32[384,128]{1,0:T(8,128)S(1)} %add_add_fusion), channel_id=1, source_target_pairs={{0,1},{1,2},{2,3},{3,0},{4,5},{5,6},{6,7},{7,4},{8,9},{9,10},{10,1... | collective-permute-start | bytes 589832 | tf_op jit(solution)/shard_map/ppermute | solution.py:88
  31.2 12.2 %collective-permute-start.4 = (f32[384,128]{1,0:T(8,128)S(1)}, f32[384,128]{1,0:T(8,128)}, u32[]{:S(2)}, u32[]{:S(2)}) collective-permute-start(f32[384,128]{1,0:T(8,128)S(1)} %add_add_fusion), channel_id=1, source_target_pairs={{0,2},{1,3},{2,0},{3,1},{4,6},{5,7},{6,4},{7,5},{8,10},{9,11},{10,... | collective-permute-start | bytes 589832 | tf_op jit(solution)/shard_map/ppermute | solution.py:88
  32.2 12.0 %collective-permute-start.5 = (f32[384,128]{1,0:T(8,128)S(1)}, f32[384,128]{1,0:T(8,128)}, u32[]{:S(2)}, u32[]{:S(2)}) collective-permute-start(f32[384,128]{1,0:T(8,128)S(1)} %add_add_fusion), channel_id=1, source_target_pairs={{0,3},{1,0},{2,1},{3,2},{4,7},{5,4},{6,5},{7,6},{8,11},{9,8},{10,9... | collective-permute-start | bytes 589832 | tf_op jit(solution)/shard_map/ppermute | solution.py:88
  34.5 10.9 %copy-start.12 = (f32[384,128]{1,0:T(8,128)S(1)}, f32[384,128]{1,0:T(8,128)}, u32[]{:S(2)}) copy-start(f32[384,128]{1,0:T(8,128)} %param.10) | copy-start | bytes 589828
  45.3 1.5 %copy-start.7 = (f32[384,128]{1,0:T(8,128)}, f32[384,128]{1,0:T(8,128)S(1)}, u32[]{:S(2)}) copy-start(f32[384,128]{1,0:T(8,128)S(1)} %get-tuple-element.12) | copy-start | bytes 589828
  45.4 1.5 %copy-start.8 = (f32[384,128]{1,0:T(8,128)}, f32[384,128]{1,0:T(8,128)S(1)}, u32[]{:S(2)}) copy-start(f32[384,128]{1,0:T(8,128)S(1)} %get-tuple-element.13) | copy-start | bytes 589828
  51.5 1.7 %copy-start.1 = (f32[2,2,2,2,2,1,8,1152]{7,6,5,4,3,2,1,0:T(8,128)}, f32[2,2,2,2,2,1,8,1152]{7,6,5,4,3,2,1,0:T(8,128)S(1)}, u32[]{:S(2)}) copy-start(f32[2,2,2,2,2,1,8,1152]{7,6,5,4,3,2,1,0:T(8,128)S(1)} %get-tuple-element.6) | copy-start | bytes 3538948
  51.5 1.7 %copy-start.3 = (f32[2,2,2,2,2,1,8,1152]{7,6,5,4,3,2,1,0:T(8,128)}, f32[2,2,2,2,2,1,8,1152]{7,6,5,4,3,2,1,0:T(8,128)S(1)}, u32[]{:S(2)}) copy-start(f32[2,2,2,2,2,1,8,1152]{7,6,5,4,3,2,1,0:T(8,128)S(1)} %get-tuple-element.7) | copy-start | bytes 3538948
  51.8 2.6 %copy-start.5 = (f32[2,2,2,2,2,1,8,1024]{7,6,5,4,3,2,1,0:T(8,128)}, f32[2,2,2,2,2,1,8,1024]{7,6,5,4,3,2,1,0:T(8,128)S(1)}, u32[]{:S(2)}) copy-start(f32[2,2,2,2,2,1,8,1024]{7,6,5,4,3,2,1,0:T(8,128)S(1)} %get-tuple-element.8) | copy-start | bytes 3145732
  51.8 2.6 %copy-start.6 = (f32[2,2,2,2,2,1,8,1024]{7,6,5,4,3,2,1,0:T(8,128)}, f32[2,2,2,2,2,1,8,1024]{7,6,5,4,3,2,1,0:T(8,128)S(1)}, u32[]{:S(2)}) copy-start(f32[2,2,2,2,2,1,8,1024]{7,6,5,4,3,2,1,0:T(8,128)S(1)} %get-tuple-element.9) | copy-start | bytes 3145732
  53.2 3.0 %collective-permute-start.12 = (f32[2,2,2,2,2,8,1024]{6,5,0,3,1,4,2:T(8,128)}, f32[2,2,2,2,2,8,1024]{6,5,0,3,1,4,2:T(8,128)}, u32[]{:S(2)}, u32[]{:S(2)}) collective-permute-start(f32[2,2,2,2,2,8,1024]{6,5,0,3,1,4,2:T(8,128)} %select_bitcast_fusion.1), channel_id=1, source_target_pairs={{0,4},{4,0},{8,12},{12,8},{16,20},{20,16},{24,28},{28,24},{32,36},... | collective-permute-start | bytes 3145736 | tf_op jit(solution)/shard_map/ppermute | solution.py:25
  54.4 6.0 %collective-permute-start.6 = (f32[2,2,2,2,2,8,1152]{6,5,0,1,3,2,4:T(8,128)}, f32[2,2,2,2,2,8,1152]{6,5,0,1,3,2,4:T(8,128)}, u32[]{:S(2)}, u32[]{:S(2)}) collective-permute-start(f32[2,2,2,2,2,8,1152]{6,5,0,1,3,2,4:T(8,128)} %select_bitcast_fusion), channel_id=1, source_target_pairs={{0,4},{4,0},{8,12},{12,8},{16,20},{20,16},{24,28},{28,24},{32,36},... | collective-permute-start | bytes 3538952 | tf_op jit(solution)/shard_map/ppermute | solution.py:25
  54.9 5.5 %copy-start.2 = (f32[2,2,2,2,2,1,8,1152]{7,6,5,4,3,2,1,0:T(8,128)S(1)}, f32[2,2,2,2,2,1,8,1152]{7,6,5,4,3,2,1,0:T(8,128)}, u32[]{:S(2)}) copy-start(f32[2,2,2,2,2,1,8,1152]{7,6,5,4,3,2,1,0:T(8,128)} %copy-done.1) | copy-start | bytes 3538948
  55.0 5.5 %copy-start.4 = (f32[2,2,2,2,2,1,8,1152]{7,6,5,4,3,2,1,0:T(8,128)S(1)}, f32[2,2,2,2,2,1,8,1152]{7,6,5,4,3,2,1,0:T(8,128)}, u32[]{:S(2)}) copy-start(f32[2,2,2,2,2,1,8,1152]{7,6,5,4,3,2,1,0:T(8,128)} %copy-done.3) | copy-start | bytes 3538948
  58.4 14.5 %collective-permute-start.13 = (f32[2,2,2,2,1,8,1024]{6,5,0,2,1,3,4:T(8,128)S(1)}, f32[2,2,2,2,1,8,1024]{6,5,0,2,1,3,4:T(8,128)S(1)}, u32[]{:S(2)}, u32[]{:S(2)}) collective-permute-start(f32[2,2,2,2,1,8,1024]{6,5,0,2,1,3,4:T(8,128)S(1)} %select_bitcast_fusion.3), channel_id=1, source_target_pairs={{0,32},{4,36},{8,40},{12,44},{16,48},{20,52},{24,56},{28,60},{32,0... | collective-permute-start | bytes 1572872 | tf_op jit(solution)/shard_map/ppermute | solution.py:25
  62.0 17.0 %collective-permute-start.7 = (f32[2,2,2,2,1,8,1152]{6,5,0,1,3,2,4:T(8,128)S(1)}, f32[2,2,2,2,1,8,1152]{6,5,0,1,3,2,4:T(8,128)S(1)}, u32[]{:S(2)}, u32[]{:S(2)}) collective-permute-start(f32[2,2,2,2,1,8,1152]{6,5,0,1,3,2,4:T(8,128)S(1)} %select_bitcast_fusion.2), channel_id=1, source_target_pairs={{0,8},{4,12},{8,0},{12,4},{16,24},{20,28},{24,16},{28,20},{32,40},... | collective-permute-start | bytes 1769480 | tf_op jit(solution)/shard_map/ppermute | solution.py:25
  73.1 10.7 %collective-permute-start.14 = (f32[2,2,1,2,1,8,1024]{6,5,0,3,1,4,2:T(8,128)S(1)}, f32[2,2,1,2,1,8,1024]{6,5,0,3,1,4,2:T(8,128)S(1)}, u32[]{:S(2)}, u32[]{:S(2)}) collective-permute-start(f32[2,2,1,2,1,8,1024]{6,5,0,3,1,4,2:T(8,128)S(1)} %select_bitcast_fusion.5), channel_id=1, source_target_pairs={{0,8},{4,12},{8,0},{12,4},{16,24},{20,28},{24,16},{28,20},{32,40},... | collective-permute-start | bytes 786440 | tf_op jit(solution)/shard_map/ppermute | solution.py:25
  83.8 9.5 %collective-permute-start.15 = (f32[2,1,2,1,1,8,1024]{6,5,0,2,4,3,1:T(8,128)S(1)}, f32[2,1,2,1,1,8,1024]{6,5,0,2,4,3,1:T(8,128)S(1)}, u32[]{:S(2)}, u32[]{:S(2)}) collective-permute-start(f32[2,1,2,1,1,8,1024]{6,5,0,2,4,3,1:T(8,128)S(1)} %select_bitcast_fusion.7), channel_id=1, source_target_pairs={{0,64},{4,68},{8,72},{12,76},{16,80},{20,84},{24,88},{28,92},{32,9... | collective-permute-start | bytes 393224 | tf_op jit(solution)/shard_map/ppermute | solution.py:25
  87.3 34.1 %copy-start.11 = (f32[8,128]{1,0:T(8,128)S(1)}, f32[8,128]{1,0:T(8,128)}, u32[]{:S(2)}) copy-start(f32[8,128]{1,0:T(8,128)} %param.15) | copy-start | bytes 12292
  87.3 34.8 %copy-start.10 = (f32[8,2048]{1,0:T(8,128)S(1)}, f32[8,2048]{1,0:T(8,128)}, u32[]{:S(2)}) copy-start(f32[8,2048]{1,0:T(8,128)} %param.14) | copy-start | bytes 196612
  87.4 11.0 %collective-permute-start.8 = (f32[2,2,2,1,1,8,1152]{6,5,0,1,2,4,3:T(8,128)S(1)}, f32[2,2,2,1,1,8,1152]{6,5,0,1,2,4,3:T(8,128)S(1)}, u32[]{:S(2)}, u32[]{:S(2)}) collective-permute-start(f32[2,2,2,1,1,8,1152]{6,5,0,1,2,4,3:T(8,128)S(1)} %select_bitcast_fusion.4), channel_id=1, source_target_pairs={{0,32},{4,36},{8,40},{12,44},{16,48},{20,52},{24,56},{28,60},{32,0... | collective-permute-start | bytes 884744 | tf_op jit(solution)/shard_map/ppermute | solution.py:25
  93.4 6.2 %collective-permute-start.16 = (f32[2,1,1,1,1,8,1024]{6,5,4,3,2,1,0:T(8,128)S(1)}, f32[2,1,1,1,1,8,1024]{6,5,4,3,2,1,0:T(8,128)S(1)}, u32[]{:S(2)}, u32[]{:S(2)}) collective-permute-start(f32[2,1,1,1,1,8,1024]{6,5,4,3,2,1,0:T(8,128)S(1)} %select_bitcast_fusion.9), channel_id=1, source_target_pairs={{0,16},{4,20},{8,24},{12,28},{16,0},{20,4},{24,8},{28,12},{32,48},... | collective-permute-start | bytes 196616 | tf_op jit(solution)/shard_map/ppermute | solution.py:25
  98.4 6.7 %collective-permute-start.9 = (f32[2,2,1,1,1,8,1152]{6,5,0,1,4,3,2:T(8,128)S(1)}, f32[2,2,1,1,1,8,1152]{6,5,0,1,4,3,2:T(8,128)S(1)}, u32[]{:S(2)}, u32[]{:S(2)}) collective-permute-start(f32[2,2,1,1,1,8,1152]{6,5,0,1,4,3,2:T(8,128)S(1)} %select_bitcast_fusion.6), channel_id=1, source_target_pairs={{0,16},{4,20},{8,24},{12,28},{16,0},{20,4},{24,8},{28,12},{32,48},... | collective-permute-start | bytes 442376 | tf_op jit(solution)/shard_map/ppermute | solution.py:25
  105.2 7.7 %collective-permute-start.10 = (f32[2,1,1,1,1,8,1152]{6,5,4,3,2,1,0:T(8,128)S(1)}, f32[2,1,1,1,1,8,1152]{6,5,4,3,2,1,0:T(8,128)S(1)}, u32[]{:S(2)}, u32[]{:S(2)}) collective-permute-start(f32[2,1,1,1,1,8,1152]{6,5,4,3,2,1,0:T(8,128)S(1)} %select_bitcast_fusion.8), channel_id=1, source_target_pairs={{0,64},{4,68},{8,72},{12,76},{16,80},{20,84},{24,88},{28,92},{32,9... | collective-permute-start | bytes 221192 | tf_op jit(solution)/shard_map/ppermute | solution.py:25
  105.3 12.5 %collective-permute-start.17 = (f32[1,1,1,1,1,8,1024]{6,5,4,3,2,1,0:T(8,128)S(1)}, f32[1,1,1,1,1,8,1024]{6,5,4,3,2,1,0:T(8,128)S(1)}, u32[]{:S(2)}, u32[]{:S(2)}) collective-permute-start(f32[1,1,1,1,1,8,1024]{6,5,4,3,2,1,0:T(8,128)S(1)} %slice_select_fusion.1), channel_id=1, source_target_pairs={{0,128},{4,132},{8,136},{12,140},{16,144},{20,148},{24,152},{28,15... | collective-permute-start | bytes 98312 | tf_op jit(solution)/shard_map/ppermute | solution.py:25
  113.0 8.5 %collective-permute-start.11 = (f32[1,1,1,1,1,8,1152]{6,5,4,3,2,1,0:T(8,128)S(1)}, f32[1,1,1,1,1,8,1152]{6,5,4,3,2,1,0:T(8,128)S(1)}, u32[]{:S(2)}, u32[]{:S(2)}) collective-permute-start(f32[1,1,1,1,1,8,1152]{6,5,4,3,2,1,0:T(8,128)S(1)} %slice_select_fusion), channel_id=1, source_target_pairs={{0,128},{4,132},{8,136},{12,140},{16,144},{20,148},{24,152},{28,15... | collective-permute-start | bytes 110600 | tf_op jit(solution)/shard_map/ppermute | solution.py:25
Sparse Core Ops, SparseCore 0:
  55.0 80.8 all-gather.1

commit v3 on v1

--- a/solution.py
+++ b/solution.py
@@ -77,14 +77,13 @@
         axis=1,
     )
 
-    partial_panel = jnp.dot(
-        panel_adj, inv_tile, precision=precise, preferred_element_type=jnp.float32
-    )
-    parts = partial_panel.reshape(partial_panel.shape[0], cols_n, col_width)
-    own = lax.dynamic_index_in_dim(parts, col_place, 1, keepdims=False)
+    def times_inv_columns(block):
+        columns = lax.dynamic_slice_in_dim(inv_tile, block * col_width, col_width, 1)
+        return jnp.dot(panel_adj, columns, precision=precise, preferred_element_type=jnp.float32)
+
+    own = times_inv_columns(col_place)
     for shift in range(1, cols_n):
-        target = jnp.maximum(col_place - shift, 0)
-        piece = lax.dynamic_index_in_dim(parts, target, 1, keepdims=False)
+        piece = times_inv_columns(jnp.maximum(col_place - shift, 0))
         own = own + lax.ppermute(piece, "col", [(c, c - shift) for c in range(shift, cols_n)])
     panel_out = own
     blocks = [None] * cols_n

time: 141 us -> 144 us (1.021)
  other arithmetic: 8.62 us -> 20.4 us
  waiting for transfers between devices: 57.2 us -> 48.8 us
  local copies, waits for them, and re-layouts: 10.1 us -> 6.14 us
  matrix products: 18 us -> 21.9 us
    ppermute x24, waiting for transfers between devices: 53.3 us -> 46.3 us  [swap_with(): return lax.ppermute(value, axis, [(i, i ^ 1 << bit) for i in range(size)])]
    dot_general x1 -> x4, matrix products: 2.85 us -> 7.18 us  [times_inv_columns(): jnp.dot(panel_adj, columns, precision=precise, preferred_element_type=jnp...]
    select_n x12, other arithmetic: 2.59 us -> 6.77 us  [all_gather_rows(): jnp.where(mine == 0, jnp.concatenate([held, other], dim), jnp.concatenate...]
    dynamic_slice x1 -> x0, local copies, waits for them, and re-layouts: 3.78 us -> none  [per_device(): piece = lax.dynamic_index_in_dim(parts, target, 1, keepdims=False)]
    concatenate x8, other arithmetic: 1.97 us -> 5.65 us  [all_gather_rows(): jnp.concatenate([held, other], dim)]
    broadcast_in_dim x8, other arithmetic: 0.79 us -> 3.4 us  [reduce_scatter_rows(): held = jnp.expand_dims(keep + swap_with(send, axis, size, bit), dim)]
    select_n x12, other arithmetic: 0.51 us -> 2.97 us  [reduce_scatter_rows(): send = jnp.where(mine == 0, high, low)]
    reshape x1 -> x0, local copies, waits for them, and re-layouts: 2.29 us -> none  [per_device(): parts = partial_panel.reshape(partial_panel.shape[0], cols_n, col_width)]
  transfers between devices with their start and end apart: 30 -> 30, of which waited for: 13 -> 13; matrix products, arithmetic and copies ran while one was open for 18% -> 30% of each run, Pallas kernels for 0% -> 0%
where the time goes in v3:
time: 144 us; the launch traced here: 143 us
  waiting for transfers between devices  48.8 us (34%)
  starting transfers between devices  44.7 us (31%)
  matrix products  21.9 us (15%)
  other arithmetic  20.4 us (14%)
  local copies, waits for them, and re-layouts  6.14 us (4%)
    ppermute x24, waiting for transfers between devices, swap_with(): return lax.ppermute(value, axis, [(i, i ^ 1 << bit) for i in range(size)])  46.3 us
    ppermute x24, starting transfers between devices, swap_with(): return lax.ppermute(value, axis, [(i, i ^ 1 << bit) for i in range(size)])  31.9 us
    ppermute x3, starting transfers between devices, per_device(): lax.ppermute(own, 'col', [(c, (c + shift) % cols_n) for c in range(cols_n)])  8.9 us
    dot_general x2, matrix products, contract_rows(): lax.dot_general(left, right, (((0,), (0,)), ((), ())), precision=lax.Prec...  7.56 us
    dot_general x4, matrix products, times_inv_columns(): jnp.dot(panel_adj, columns, precision=precise, preferred_element_type=jnp...  7.18 us
    dot_general x1, matrix products, per_device(): jnp.dot(scaled, gathered, precision=precise, preferred_element_type=jnp.f...  7.15 us
    select_n x12, other arithmetic, all_gather_rows(): jnp.where(mine == 0, jnp.concatenate([held, other], dim), jnp.concatenate...  6.77 us
    concatenate x8, other arithmetic, all_gather_rows(): jnp.concatenate([held, other], dim)  5.65 us
  transfers between devices with their start and end apart: 30, of which 13 were waited for; matrix products, arithmetic and copies ran while one was open for 30% of the time, Pallas kernels for 0%

profile of v3, /device:TPU:24, one launch (start us, length us, event | category | flops | bytes accessed | tf_op | source)
XLA Modules:
  0.0 143.2 jit_solution(7739617757056025611)
XLA Ops:
  0.7 1.5 %convolution_bitcast_fusion.2 = f32[384,128]{0,1:T(8,128)S(1)} fusion(f32[384,128]{1,0:T(8,128)} %param.8, f32[128,512]{1,0:T(8,128)} %param.9, s32[]{:T(128)S(6)} %select_n.773), kind=kOutput, calls=%fused_computation.13 | convolution fusion | flops 75497472 | bytes 458756 | tf_op jit(solution)/shard_map/dot_general | solution.py:82
  3.5 2.0 %convolution_bitcast_fusion.1 = f32[384,128]{0,1:T(8,128)} fusion(f32[384,128]{1,0:T(8,128)} %param.8, f32[128,512]{1,0:T(8,128)} %param.9, s32[]{:T(128)S(6)} %select_n.774), kind=kOutput, calls=%fused_computation.12 | convolution fusion | flops 75497472 | bytes 458756 | tf_op jit(solution)/shard_map/dot_general | solution.py:82
  6.9 2.0 %convolution_bitcast_fusion = f32[384,128]{0,1:T(8,128)} fusion(f32[384,128]{1,0:T(8,128)} %param.8, f32[128,512]{1,0:T(8,128)} %param.9, s32[]{:T(128)S(6)} %select_n.775), kind=kOutput, calls=%fused_computation.11 | convolution fusion | flops 75497472 | bytes 458756 | tf_op jit(solution)/shard_map/dot_general | solution.py:82
  10.2 1.4 slice_bitcast_fusion.3
  11.6 7.2 %collective-permute-start.6 = (f32[1,1,1,1,1,1,8,1024]{7,6,5,4,3,2,1,0:T(8,128)}, f32[1,1,1,1,1,1,8,1024]{7,6,5,4,3,2,1,0:T(8,128)}, u32[]{:S(2)}, u32[]{:S(2)}) collective-permute-start(f32[1,1,1,1,1,1,8,1024]{7,6,5,4,3,2,1,0:T(8,128)} %get-tuple-element.39), channel_id=1, source_target_pairs={{0,128},{4,132},{8,136},{12,140},{16,144},{20,148},{24,152},{28,15... | collective-permute-start | bytes 98312 | tf_op jit(solution)/shard_map/ppermute | solution.py:25
  18.8 2.2 %collective-permute-done.6 = f32[1,1,1,1,1,1,8,1024]{7,6,5,4,3,2,1,0:T(8,128)} collective-permute-done((f32[1,1,1,1,1,1,8,1024]{7,6,5,4,3,2,1,0:T(8,128)}, f32[1,1,1,1,1,1,8,1024]{7,6,5,4,3,2,1,0:T(8,128)}, u32[]{:S(2)}, u32[]{:S(2)}) %collective-permute-start.6) | collective-permute-done | bytes 32800 | tf_op jit(solution)/shard_map/ppermute | solution.py:25
  21.9 2.2 %collective-permute-start.7 = (f32[2,1,1,1,1,1,8,1024]{7,6,0,5,4,3,2,1:T(8,128)S(1)}, f32[2,1,1,1,1,1,8,1024]{7,6,0,5,4,3,2,1:T(8,128)S(1)}, u32[]{:S(2)}, u32[]{:S(2)}) collective-permute-start(f32[2,1,1,1,1,1,8,1024]{7,6,0,5,4,3,2,1:T(8,128)S(1)} %fusion.25), channel_id=1, source_target_pairs={{0,64},{4,68},{8,72},{12,76},{16,80},{20,84},{24,88},{28,92},{32,9... | collective-permute-start | bytes 196616 | tf_op jit(solution)/shard_map/ppermute | solution.py:25
  24.1 3.2 %collective-permute-done.12 = f32[1,1,1,1,1,1,8,1024]{7,6,5,4,3,2,1,0:T(8,128)} collective-permute-done((f32[1,1,1,1,1,1,8,1024]{7,6,5,4,3,2,1,0:T(8,128)}, f32[1,1,1,1,1,1,8,1024]{7,6,5,4,3,2,1,0:T(8,128)}, u32[]{:S(2)}, u32[]{:S(2)}) %collective-permute-start.12) | collective-permute-done | bytes 32800 | tf_op jit(solution)/shard_map/ppermute | solution.py:25
  31.2 2.4 %collective-permute-start.8 = (f32[2,2,1,1,1,1,8,1024]{7,6,1,0,5,4,3,2:T(8,128)S(1)}, f32[2,2,1,1,1,1,8,1024]{7,6,1,0,5,4,3,2:T(8,128)S(1)}, u32[]{:S(2)}, u32[]{:S(2)}) collective-permute-start(f32[2,2,1,1,1,1,8,1024]{7,6,1,0,5,4,3,2:T(8,128)S(1)} %copy.56), channel_id=1, source_target_pairs={{0,16},{4,20},{8,24},{12,28},{16,0},{20,4},{24,8},{28,12},{32,48},... | collective-permute-start | bytes 393224 | tf_op jit(solution)/shard_map/ppermute | solution.py:25
  34.3 1.5 %collective-permute-start.14 = (f32[2,1,1,2,1,1,8,1024]{7,6,5,4,3,2,1,0:T(8,128)S(1)}, f32[2,1,1,2,1,1,8,1024]{7,6,5,4,3,2,1,0:T(8,128)S(1)}, u32[]{:S(2)}, u32[]{:S(2)}) collective-permute-start(f32[2,1,1,2,1,1,8,1024]{7,6,5,4,3,2,1,0:T(8,128)S(1)} %maximum_select_fusion.15), channel_id=1, source_target_pairs={{0,64},{4,68},{8,72},{12,76},{16,80},{20,84},{24,88},{28,92},{32,9... | collective-permute-start | bytes 393224 | tf_op jit(solution)/shard_map/ppermute | solution.py:25
  36.0 1.6 %fusion.10 = f32[384,128]{0,1:T(8,128)S(1)} fusion(f32[384,128]{0,1:T(8,128)} %collective-permute-done.2, f32[384,128]{0,1:T(8,128)} %collective-permute-done.1, f32[384,128]{0,1:T(8,128)} %collective-permute-done, f32[384,128]{1,0:T(8,128)S(1)} %copy-done.10, f32[128,512]{1,0:T(8,128)} %param.9, s32[]{:T(128)S(6)} %select_n.772), kind=kOutput, calls=%fused_computation.17 | convolution fusion | flops 75644928 | bytes 1048580 | tf_op jit(solution)/shard_map/dot_general | solution.py:82
  37.5 2.7 %collective-permute-start.3 = (f32[384,128]{0,1:T(8,128)S(1)}, f32[384,128]{0,1:T(8,128)S(1)}, u32[]{:S(2)}, u32[]{:S(2)}) collective-permute-start(f32[384,128]{0,1:T(8,128)S(1)} %fusion.10), channel_id=1, source_target_pairs={{0,1},{1,2},{2,3},{3,0},{4,5},{5,6},{6,7},{7,4},{8,9},{9,10},{10,1... | collective-permute-start | bytes 589832 | tf_op jit(solution)/shard_map/ppermute | solution.py:94
  40.3 6.2 %collective-permute-start.4 = (f32[384,128]{0,1:T(8,128)S(1)}, f32[384,128]{0,1:T(8,128)S(1)}, u32[]{:S(2)}, u32[]{:S(2)}) collective-permute-start(f32[384,128]{0,1:T(8,128)S(1)} %fusion.10), channel_id=1, source_target_pairs={{0,2},{1,3},{2,0},{3,1},{4,6},{5,7},{6,4},{7,5},{8,10},{9,11},{10,... | collective-permute-start | bytes 589832 | tf_op jit(solution)/shard_map/ppermute | solution.py:94
  49.7 2.5 %collective-permute-done.4 = f32[384,128]{0,1:T(8,128)S(1)} collective-permute-done((f32[384,128]{0,1:T(8,128)S(1)}, f32[384,128]{0,1:T(8,128)S(1)}, u32[]{:S(2)}, u32[]{:S(2)}) %collective-permute-start.4) | collective-permute-done | bytes 196640 | tf_op jit(solution)/shard_map/ppermute | solution.py:94
  53.3 6.8 %fusion.21 = f32[512,2048]{1,0:T(8,128)S(1)} fusion(f32[384,2048]{1,0:T(8,128)S(1)} %copy-done, f32[384,128]{0,1:T(8,128)S(1)} %get-tuple-element.23, f32[384,128]{0,1:T(8,128)S(1)} %get-tuple-element.24, f32[384,128]{0,1:T(8,128)S(1)} %get-tuple-element.25, f32[384,128]{0,1:T(8,128)S(1)} %get-tuple-element.22), kind=kOutput, calls=%fused_computation.59 | convolution fusion | flops 4832428032 | bytes 8126464 | tf_op jit(solution)/shard_map/dot_general | solution.py:8
  61.3 1.6 %select_bitcast_fusion.1 = f32[2,2,2,2,2,8,1024]{6,5,0,3,1,4,2:T(8,128)} fusion(f32[2,2,2,2,2,1,8,1024]{7,6,5,4,3,2,1,0:T(8,128)S(1)} %get-tuple-element.21, f32[2,2,2,2,2,1,8,1024]{7,6,5,4,3,2,1,0:T(8,128)S(1)} %get-tuple-element.20, pred[]{:T(512)S(6)} %eq.17), kind=kLoop, calls=%fused_computation.22 | loop fusion | flops 262144 | bytes 3145729 | tf_op jit(solution)/shard_map/jit(_where)/select_n | solution.py:39
  67.2 1.7 %copy.79 = f32[384,128]{1,0:T(8,128)} copy(f32[384,128]{0,1:T(8,128)} %copy-done.11) | data formatting | bytes 393216
  71.3 7.2 %collective-permute-done.10 = f32[2,2,2,2,1,1,8,1024]{7,6,5,4,3,2,1,0:T(8,128)} collective-permute-done((f32[2,2,2,2,1,1,8,1024]{7,6,5,4,3,2,1,0:T(8,128)}, f32[2,2,2,2,1,1,8,1024]{7,6,5,4,3,2,1,0:T(8,128)}, u32[]{:S(2)}, u32[]{:S(2)}) %collective-permute-start.10) | collective-permute-done | bytes 524320 | tf_op jit(solution)/shard_map/ppermute | solution.py:25
  82.0 1.5 %fusion.11 = f32[2,2,2,2,2,1,8,1024]{7,6,0,3,1,4,5,2:T(8,128)S(1)} fusion(f32[2,2,2,2,2,8,1024]{6,5,0,3,1,4,2:T(8,128)} %collective-permute-done.24, f32[2,2,2,2,2,1,8,1024]{7,6,5,4,3,2,1,0:T(8,128)S(1)} %copy-done.8, f32[2,2,2,2,2,1,8,1024]{7,6,5,4,3,2,1,0:T(8,128)S(1)} %copy-done.6, pred[]{:T(512)S(6)} %eq.17), kind=kLoop, calls=%fused_computation.21 | loop fusion | flops 524288 | bytes 4194305 | tf_op jit(solution)/shard_map/broadcast_in_dim | solution.py:40
  84.7 1.5 %fusion.7 = f32[2,2,2,2,2,1,8,1152]{7,6,0,1,3,2,5,4:T(8,128)S(1)} fusion(f32[2,2,2,2,2,8,1152]{6,5,0,1,3,2,4:T(8,128)} %collective-permute-done.18, f32[2,2,2,2,2,1,8,1152]{7,6,5,4,3,2,1,0:T(8,128)S(1)} %copy-done.4, f32[2,2,2,2,2,1,8,1152]{7,6,5,4,3,2,1,0:T(8,128)S(1)} %copy-done.2, pred[]{:T(512)S(6)} %eq.17), kind=kLoop, calls=%fused_computation.9 | loop fusion | flops 589824 | bytes 4718593 | tf_op jit(solution)/shard_map/broadcast_in_dim | solution.py:40
  87.4 10.4 %collective-permute-done.25 = f32[2,2,2,2,1,8,1024]{6,5,0,2,1,3,4:T(8,128)S(1)} collective-permute-done((f32[2,2,2,2,1,8,1024]{6,5,0,2,1,3,4:T(8,128)S(1)}, f32[2,2,2,2,1,8,1024]{6,5,0,2,1,3,4:T(8,128)S(1)}, u32[]{:S(2)}, u32[]{:S(2)}) %collective-permute-start.25) | collective-permute-done | bytes 524320 | tf_op jit(solution)/shard_map/ppermute | solution.py:25
  99.7 1.5 %copy-done.9 = f32[384,2048]{1,0:T(8,128)S(1)} copy-done((f32[384,2048]{1,0:T(8,128)S(1)}, f32[384,2048]{1,0:T(8,128)}, u32[]{:S(2)}) %copy-start.9) | copy-done | bytes 3145752
  101.4 7.2 %fusion.4 = f32[384,2048]{1,0:T(8,128)} fusion(f32[384,2048]{1,0:T(8,128)S(1)} %copy-done.9, f32[512,1024]{1,0:T(8,128)S(1)} %bitcast.183, f32[512,1024]{1,0:T(8,128)S(1)} %bitcast.181, f32[384,128]{0,1:T(8,128)S(1)} %copy-done.15, f32[384,128]{0,1:T(8,128)S(1)} %copy-done.17, f32[384,128]{0,1:T(8,128)S(1)} %copy-done.19, f32[384,128]{0,1:T(8,128)S(1)} %copy-done.13), kind=kOutput, calls=%fused_computation.4 | convolution fusion | flops 4834263040 | bytes 11272192 | tf_op jit(solution)/shard_map/dot_general | solution.py:103
  108.8 1.5 %collective-permute-start.27 = (f32[2,1,2,1,1,8,1024]{6,5,0,2,4,3,1:T(8,128)S(1)}, f32[2,1,2,1,1,8,1024]{6,5,0,2,4,3,1:T(8,128)S(1)}, u32[]{:S(2)}, u32[]{:S(2)}) collective-permute-start(f32[2,1,2,1,1,8,1024]{6,5,0,2,4,3,1:T(8,128)S(1)} %select_bitcast_fusion.7), channel_id=1, source_target_pairs={{0,64},{4,68},{8,72},{12,76},{16,80},{20,84},{24,88},{28,92},{32,9... | collective-permute-start | bytes 393224 | tf_op jit(solution)/shard_map/ppermute | solution.py:25
  111.6 5.5 %collective-permute-done.27 = f32[2,1,2,1,1,8,1024]{6,5,0,2,4,3,1:T(8,128)S(1)} collective-permute-done((f32[2,1,2,1,1,8,1024]{6,5,0,2,4,3,1:T(8,128)S(1)}, f32[2,1,2,1,1,8,1024]{6,5,0,2,4,3,1:T(8,128)S(1)}, u32[]{:S(2)}, u32[]{:S(2)}) %collective-permute-start.27) | collective-permute-done | bytes 131104 | tf_op jit(solution)/shard_map/ppermute | solution.py:25
  117.8 2.8 %collective-permute-done.20 = f32[2,2,2,1,1,8,1152]{6,5,0,1,2,4,3:T(8,128)S(1)} collective-permute-done((f32[2,2,2,1,1,8,1152]{6,5,0,1,2,4,3:T(8,128)S(1)}, f32[2,2,2,1,1,8,1152]{6,5,0,1,2,4,3:T(8,128)S(1)}, u32[]{:S(2)}, u32[]{:S(2)}) %collective-permute-start.20) | collective-permute-done | bytes 294944 | tf_op jit(solution)/shard_map/ppermute | solution.py:25
  121.4 1.7 %collective-permute-done.28 = f32[2,1,1,1,1,8,1024]{6,5,4,3,2,1,0:T(8,128)S(1)} collective-permute-done((f32[2,1,1,1,1,8,1024]{6,5,4,3,2,1,0:T(8,128)S(1)}, f32[2,1,1,1,1,8,1024]{6,5,4,3,2,1,0:T(8,128)S(1)}, u32[]{:S(2)}, u32[]{:S(2)}) %collective-permute-start.28) | collective-permute-done | bytes 65568 | tf_op jit(solution)/shard_map/ppermute | solution.py:25
  123.0 4.4 %collective-permute-done.21 = f32[2,2,1,1,1,8,1152]{6,5,0,1,4,3,2:T(8,128)S(1)} collective-permute-done((f32[2,2,1,1,1,8,1152]{6,5,0,1,4,3,2:T(8,128)S(1)}, f32[2,2,1,1,1,8,1152]{6,5,0,1,4,3,2:T(8,128)S(1)}, u32[]{:S(2)}, u32[]{:S(2)}) %collective-permute-start.21) | collective-permute-done | bytes 147488 | tf_op jit(solution)/shard_map/ppermute | solution.py:25
  128.6 2.4 %collective-permute-start.29 = (f32[1,1,1,1,1,8,1024]{6,5,4,3,2,1,0:T(8,128)S(1)}, f32[1,1,1,1,1,8,1024]{6,5,4,3,2,1,0:T(8,128)S(1)}, u32[]{:S(2)}, u32[]{:S(2)}) collective-permute-start(f32[1,1,1,1,1,8,1024]{6,5,4,3,2,1,0:T(8,128)S(1)} %slice_select_fusion.1), channel_id=1, source_target_pairs={{0,128},{4,132},{8,136},{12,140},{16,144},{20,148},{24,152},{28,15... | collective-permute-start | bytes 98312 | tf_op jit(solution)/shard_map/ppermute | solution.py:25
  131.0 2.8 %collective-permute-done.22 = f32[2,1,1,1,1,8,1152]{6,5,4,3,2,1,0:T(8,128)S(1)} collective-permute-done((f32[2,1,1,1,1,8,1152]{6,5,4,3,2,1,0:T(8,128)S(1)}, f32[2,1,1,1,1,8,1152]{6,5,4,3,2,1,0:T(8,128)S(1)}, u32[]{:S(2)}, u32[]{:S(2)}) %collective-permute-start.22) | collective-permute-done | bytes 73760 | tf_op jit(solution)/shard_map/ppermute | solution.py:25
  133.9 2.6 %collective-permute-start.23 = (f32[1,1,1,1,1,8,1152]{6,5,4,3,2,1,0:T(8,128)S(1)}, f32[1,1,1,1,1,8,1152]{6,5,4,3,2,1,0:T(8,128)S(1)}, u32[]{:S(2)}, u32[]{:S(2)}) collective-permute-start(f32[1,1,1,1,1,8,1152]{6,5,4,3,2,1,0:T(8,128)S(1)} %slice_select_fusion), channel_id=1, source_target_pairs={{0,128},{4,132},{8,136},{12,140},{16,144},{20,148},{24,152},{28,15... | collective-permute-start | bytes 110600 | tf_op jit(solution)/shard_map/ppermute | solution.py:25
  136.6 5.3 %collective-permute-done.23 = f32[1,1,1,1,1,8,1152]{6,5,4,3,2,1,0:T(8,128)S(1)} collective-permute-done((f32[1,1,1,1,1,8,1152]{6,5,4,3,2,1,0:T(8,128)S(1)}, f32[1,1,1,1,1,8,1152]{6,5,4,3,2,1,0:T(8,128)S(1)}, u32[]{:S(2)}, u32[]{:S(2)}) %collective-permute-start.23) | collective-permute-done | bytes 36896 | tf_op jit(solution)/shard_map/ppermute | solution.py:25
  (142 shorter events, 34.8 us)
Async XLA Ops:
  0.6 52.6 %copy-start = (f32[384,2048]{1,0:T(8,128)S(1)}, f32[384,2048]{1,0:T(8,128)}, u32[]{:S(2)}) copy-start(f32[384,2048]{1,0:T(8,128)} %param.12) | copy-start | bytes 9437188
  0.7 35.3 %copy-start.10 = (f32[384,128]{1,0:T(8,128)S(1)}, f32[384,128]{1,0:T(8,128)}, u32[]{:S(2)}) copy-start(f32[384,128]{1,0:T(8,128)} %param.8) | copy-start | bytes 589828
  2.2 33.7 %collective-permute-start = (f32[384,128]{0,1:T(8,128)S(1)}, f32[384,128]{0,1:T(8,128)}, u32[]{:S(2)}, u32[]{:S(2)}) collective-permute-start(f32[384,128]{0,1:T(8,128)S(1)} %convolution_bitcast_fusion.2), channel_id=1, source_target_pairs={{1,0},{2,1},{3,2},{5,4},{6,5},{7,6},{9,8},{10,9},{11,10},{13,12},{... | collective-permute-start | bytes 589832 | tf_op jit(solution)/shard_map/ppermute | solution.py:87
  5.6 30.4 %collective-permute-start.1 = (f32[384,128]{0,1:T(8,128)}, f32[384,128]{0,1:T(8,128)}, u32[]{:S(2)}, u32[]{:S(2)}) collective-permute-start(f32[384,128]{0,1:T(8,128)} %convolution_bitcast_fusion.1), channel_id=1, source_target_pairs={{2,0},{3,1},{6,4},{7,5},{10,8},{11,9},{14,12},{15,13},{18,16},{19,... | collective-permute-start | bytes 589832 | tf_op jit(solution)/shard_map/ppermute | solution.py:87
  8.9 27.1 %collective-permute-start.2 = (f32[384,128]{0,1:T(8,128)}, f32[384,128]{0,1:T(8,128)}, u32[]{:S(2)}, u32[]{:S(2)}) collective-permute-start(f32[384,128]{0,1:T(8,128)} %convolution_bitcast_fusion), channel_id=1, source_target_pairs={{3,0},{7,4},{11,8},{15,12},{19,16},{23,20},{27,24},{31,28},{35,32}... | collective-permute-start | bytes 589832 | tf_op jit(solution)/shard_map/ppermute | solution.py:87
  11.6 9.4 %collective-permute-start.6 = (f32[1,1,1,1,1,1,8,1024]{7,6,5,4,3,2,1,0:T(8,128)}, f32[1,1,1,1,1,1,8,1024]{7,6,5,4,3,2,1,0:T(8,128)}, u32[]{:S(2)}, u32[]{:S(2)}) collective-permute-start(f32[1,1,1,1,1,1,8,1024]{7,6,5,4,3,2,1,0:T(8,128)} %get-tuple-element.39), channel_id=1, source_target_pairs={{0,128},{4,132},{8,136},{12,140},{16,144},{20,148},{24,152},{28,15... | collective-permute-start | bytes 98312 | tf_op jit(solution)/shard_map/ppermute | solution.py:25
  18.8 8.4 %collective-permute-start.12 = (f32[1,1,1,1,1,1,8,1024]{7,6,5,4,3,2,1,0:T(8,128)}, f32[1,1,1,1,1,1,8,1024]{7,6,5,4,3,2,1,0:T(8,128)}, u32[]{:S(2)}, u32[]{:S(2)}) collective-permute-start(f32[1,1,1,1,1,1,8,1024]{7,6,5,4,3,2,1,0:T(8,128)} %get-tuple-element.40), channel_id=1, source_target_pairs={{0,128},{4,132},{8,136},{12,140},{16,144},{20,148},{24,152},{28,15... | collective-permute-start | bytes 98312 | tf_op jit(solution)/shard_map/ppermute | solution.py:25
  21.9 9.3 %collective-permute-start.7 = (f32[2,1,1,1,1,1,8,1024]{7,6,0,5,4,3,2,1:T(8,128)S(1)}, f32[2,1,1,1,1,1,8,1024]{7,6,0,5,4,3,2,1:T(8,128)S(1)}, u32[]{:S(2)}, u32[]{:S(2)}) collective-permute-start(f32[2,1,1,1,1,1,8,1024]{7,6,0,5,4,3,2,1:T(8,128)S(1)} %fusion.25), channel_id=1, source_target_pairs={{0,64},{4,68},{8,72},{12,76},{16,80},{20,84},{24,88},{28,92},{32,9... | collective-permute-start | bytes 196616 | tf_op jit(solution)/shard_map/ppermute | solution.py:25
  28.1 6.2 %collective-permute-start.13 = (f32[2,1,1,1,1,1,8,1024]{7,6,5,4,3,2,1,0:T(8,128)S(1)}, f32[2,1,1,1,1,1,8,1024]{7,6,5,4,3,2,1,0:T(8,128)S(1)}, u32[]{:S(2)}, u32[]{:S(2)}) collective-permute-start(f32[2,1,1,1,1,1,8,1024]{7,6,5,4,3,2,1,0:T(8,128)S(1)} %maximum_select_fusion.19), channel_id=1, source_target_pairs={{0,16},{4,20},{8,24},{12,28},{16,0},{20,4},{24,8},{28,12},{32,48},... | collective-permute-start | bytes 196616 | tf_op jit(solution)/shard_map/ppermute | solution.py:25
  31.2 15.3 %collective-permute-start.8 = (f32[2,2,1,1,1,1,8,1024]{7,6,1,0,5,4,3,2:T(8,128)S(1)}, f32[2,2,1,1,1,1,8,1024]{7,6,1,0,5,4,3,2:T(8,128)S(1)}, u32[]{:S(2)}, u32[]{:S(2)}) collective-permute-start(f32[2,2,1,1,1,1,8,1024]{7,6,1,0,5,4,3,2:T(8,128)S(1)} %copy.56), channel_id=1, source_target_pairs={{0,16},{4,20},{8,24},{12,28},{16,0},{20,4},{24,8},{28,12},{32,48},... | collective-permute-start | bytes 393224 | tf_op jit(solution)/shard_map/ppermute | solution.py:25
  34.3 13.3 %collective-permute-start.14 = (f32[2,1,1,2,1,1,8,1024]{7,6,5,4,3,2,1,0:T(8,128)S(1)}, f32[2,1,1,2,1,1,8,1024]{7,6,5,4,3,2,1,0:T(8,128)S(1)}, u32[]{:S(2)}, u32[]{:S(2)}) collective-permute-start(f32[2,1,1,2,1,1,8,1024]{7,6,5,4,3,2,1,0:T(8,128)S(1)} %maximum_select_fusion.15), channel_id=1, source_target_pairs={{0,64},{4,68},{8,72},{12,76},{16,80},{20,84},{24,88},{28,92},{32,9... | collective-permute-start | bytes 393224 | tf_op jit(solution)/shard_map/ppermute | solution.py:25
  37.5 12.2 %collective-permute-start.3 = (f32[384,128]{0,1:T(8,128)S(1)}, f32[384,128]{0,1:T(8,128)S(1)}, u32[]{:S(2)}, u32[]{:S(2)}) collective-permute-start(f32[384,128]{0,1:T(8,128)S(1)} %fusion.10), channel_id=1, source_target_pairs={{0,1},{1,2},{2,3},{3,0},{4,5},{5,6},{6,7},{7,4},{8,9},{9,10},{10,1... | collective-permute-start | bytes 589832 | tf_op jit(solution)/shard_map/ppermute | solution.py:94
  40.3 11.9 %collective-permute-start.4 = (f32[384,128]{0,1:T(8,128)S(1)}, f32[384,128]{0,1:T(8,128)S(1)}, u32[]{:S(2)}, u32[]{:S(2)}) collective-permute-start(f32[384,128]{0,1:T(8,128)S(1)} %fusion.10), channel_id=1, source_target_pairs={{0,2},{1,3},{2,0},{3,1},{4,6},{5,7},{6,4},{7,5},{8,10},{9,11},{10,... | collective-permute-start | bytes 589832 | tf_op jit(solution)/shard_map/ppermute | solution.py:94
  46.4 5.8 %collective-permute-start.5 = (f32[384,128]{0,1:T(8,128)S(1)}, f32[384,128]{0,1:T(8,128)S(1)}, u32[]{:S(2)}, u32[]{:S(2)}) collective-permute-start(f32[384,128]{0,1:T(8,128)S(1)} %fusion.10), channel_id=1, source_target_pairs={{0,3},{1,0},{2,1},{3,2},{4,7},{5,4},{6,5},{7,6},{8,11},{9,8},{10,9... | collective-permute-start | bytes 589832 | tf_op jit(solution)/shard_map/ppermute | solution.py:94
  46.5 16.4 %collective-permute-start.9 = (f32[2,2,1,2,1,1,8,1024]{7,6,5,4,3,2,1,0:T(8,128)S(1)}, f32[2,2,1,2,1,1,8,1024]{7,6,5,4,3,2,1,0:T(8,128)S(1)}, u32[]{:S(2)}, u32[]{:S(2)}) collective-permute-start(f32[2,2,1,2,1,1,8,1024]{7,6,5,4,3,2,1,0:T(8,128)S(1)} %copy.57), channel_id=1, source_target_pairs={{0,32},{4,36},{8,40},{12,44},{16,48},{20,52},{24,56},{28,60},{32,0... | collective-permute-start | bytes 786440 | tf_op jit(solution)/shard_map/ppermute | solution.py:25
  47.6 16.6 %collective-permute-start.15 = (f32[2,2,1,2,1,1,8,1024]{7,6,5,4,3,2,1,0:T(8,128)S(1)}, f32[2,2,1,2,1,1,8,1024]{7,6,5,4,3,2,1,0:T(8,128)S(1)}, u32[]{:S(2)}, u32[]{:S(2)}) collective-permute-start(f32[2,2,1,2,1,1,8,1024]{7,6,5,4,3,2,1,0:T(8,128)S(1)} %maximum_select_fusion.11), channel_id=1, source_target_pairs={{0,8},{4,12},{8,0},{12,4},{16,24},{20,28},{24,16},{28,20},{32,40},... | collective-permute-start | bytes 786440 | tf_op jit(solution)/shard_map/ppermute | solution.py:25
  62.9 19.1 %collective-permute-start.24 = (f32[2,2,2,2,2,8,1024]{6,5,0,3,1,4,2:T(8,128)}, f32[2,2,2,2,2,8,1024]{6,5,0,3,1,4,2:T(8,128)}, u32[]{:S(2)}, u32[]{:S(2)}) collective-permute-start(f32[2,2,2,2,2,8,1024]{6,5,0,3,1,4,2:T(8,128)} %select_bitcast_fusion.1), channel_id=1, source_target_pairs={{0,4},{4,0},{8,12},{12,8},{16,20},{20,16},{24,28},{28,24},{32,36},... | collective-permute-start | bytes 3145736 | tf_op jit(solution)/shard_map/ppermute | solution.py:25
  63.8 14.7 %collective-permute-start.10 = (f32[2,2,2,2,1,1,8,1024]{7,6,5,4,3,2,1,0:T(8,128)}, f32[2,2,2,2,1,1,8,1024]{7,6,5,4,3,2,1,0:T(8,128)}, u32[]{:S(2)}, u32[]{:S(2)}) collective-permute-start(f32[2,2,2,2,1,1,8,1024]{7,6,5,4,3,2,1,0:T(8,128)} %maximum_select_fusion.5), channel_id=1, source_target_pairs={{0,8},{4,12},{8,0},{12,4},{16,24},{20,28},{24,16},{28,20},{32,40},... | collective-permute-start | bytes 1572872 | tf_op jit(solution)/shard_map/ppermute | solution.py:25
  65.1 14.8 %collective-permute-start.16 = (f32[2,2,1,2,2,1,8,1024]{7,6,5,4,3,2,1,0:T(8,128)}, f32[2,2,1,2,2,1,8,1024]{7,6,5,4,3,2,1,0:T(8,128)}, u32[]{:S(2)}, u32[]{:S(2)}) collective-permute-start(f32[2,2,1,2,2,1,8,1024]{7,6,5,4,3,2,1,0:T(8,128)} %maximum_select_fusion.7), channel_id=1, source_target_pairs={{0,32},{4,36},{8,40},{12,44},{16,48},{20,52},{24,56},{28,60},{32,0... | collective-permute-start | bytes 1572872 | tf_op jit(solution)/shard_map/ppermute | solution.py:25
  67.2 17.6 %collective-permute-start.18 = (f32[2,2,2,2,2,8,1152]{6,5,0,1,3,2,4:T(8,128)}, f32[2,2,2,2,2,8,1152]{6,5,0,1,3,2,4:T(8,128)}, u32[]{:S(2)}, u32[]{:S(2)}) collective-permute-start(f32[2,2,2,2,2,8,1152]{6,5,0,1,3,2,4:T(8,128)} %select_bitcast_fusion), channel_id=1, source_target_pairs={{0,4},{4,0},{8,12},{12,8},{16,20},{20,16},{24,28},{28,24},{32,36},... | collective-permute-start | bytes 3538952 | tf_op jit(solution)/shard_map/ppermute | solution.py:25
  79.8 19.3 %collective-permute-start.11 = (f32[2,2,2,2,2,1,8,1024]{7,6,5,4,3,2,1,0:T(8,128)S(1)}, f32[2,2,2,2,2,1,8,1024]{7,6,5,4,3,2,1,0:T(8,128)S(1)}, u32[]{:S(2)}, u32[]{:S(2)}) collective-permute-start(f32[2,2,2,2,2,1,8,1024]{7,6,5,4,3,2,1,0:T(8,128)S(1)} %maximum_select_fusion.2), channel_id=1, source_target_pairs={{0,4},{4,0},{8,12},{12,8},{16,20},{20,16},{24,28},{28,24},{32,36},... | collective-permute-start | bytes 3145736 | tf_op jit(solution)/shard_map/ppermute | solution.py:25
  81.2 18.2 %collective-permute-start.17 = (f32[2,2,2,2,2,1,8,1024]{7,6,5,4,3,2,1,0:T(8,128)S(1)}, f32[2,2,2,2,2,1,8,1024]{7,6,5,4,3,2,1,0:T(8,128)S(1)}, u32[]{:S(2)}, u32[]{:S(2)}) collective-permute-start(f32[2,2,2,2,2,1,8,1024]{7,6,5,4,3,2,1,0:T(8,128)S(1)} %maximum_select_fusion.3), channel_id=1, source_target_pairs={{0,4},{4,0},{8,12},{12,8},{16,20},{20,16},{24,28},{28,24},{32,36},... | collective-permute-start | bytes 3145736 | tf_op jit(solution)/shard_map/ppermute | solution.py:25
  83.6 14.1 %collective-permute-start.25 = (f32[2,2,2,2,1,8,1024]{6,5,0,2,1,3,4:T(8,128)S(1)}, f32[2,2,2,2,1,8,1024]{6,5,0,2,1,3,4:T(8,128)S(1)}, u32[]{:S(2)}, u32[]{:S(2)}) collective-permute-start(f32[2,2,2,2,1,8,1024]{6,5,0,2,1,3,4:T(8,128)S(1)} %select_bitcast_fusion.3), channel_id=1, source_target_pairs={{0,32},{4,36},{8,40},{12,44},{16,48},{20,52},{24,56},{28,60},{32,0... | collective-permute-start | bytes 1572872 | tf_op jit(solution)/shard_map/ppermute | solution.py:25
  86.3 22.3 %collective-permute-start.19 = (f32[2,2,2,2,1,8,1152]{6,5,0,1,3,2,4:T(8,128)S(1)}, f32[2,2,2,2,1,8,1152]{6,5,0,1,3,2,4:T(8,128)S(1)}, u32[]{:S(2)}, u32[]{:S(2)}) collective-permute-start(f32[2,2,2,2,1,8,1152]{6,5,0,1,3,2,4:T(8,128)S(1)} %select_bitcast_fusion.2), channel_id=1, source_target_pairs={{0,8},{4,12},{8,0},{12,4},{16,24},{20,28},{24,16},{28,20},{32,40},... | collective-permute-start | bytes 1769480 | tf_op jit(solution)/shard_map/ppermute | solution.py:25
  97.9 10.8 %collective-permute-start.26 = (f32[2,2,1,2,1,8,1024]{6,5,0,3,1,4,2:T(8,128)S(1)}, f32[2,2,1,2,1,8,1024]{6,5,0,3,1,4,2:T(8,128)S(1)}, u32[]{:S(2)}, u32[]{:S(2)}) collective-permute-start(f32[2,2,1,2,1,8,1024]{6,5,0,3,1,4,2:T(8,128)S(1)} %select_bitcast_fusion.5), channel_id=1, source_target_pairs={{0,8},{4,12},{8,0},{12,4},{16,24},{20,28},{24,16},{28,20},{32,40},... | collective-permute-start | bytes 786440 | tf_op jit(solution)/shard_map/ppermute | solution.py:25
  108.8 8.4 %collective-permute-start.27 = (f32[2,1,2,1,1,8,1024]{6,5,0,2,4,3,1:T(8,128)S(1)}, f32[2,1,2,1,1,8,1024]{6,5,0,2,4,3,1:T(8,128)S(1)}, u32[]{:S(2)}, u32[]{:S(2)}) collective-permute-start(f32[2,1,2,1,1,8,1024]{6,5,0,2,4,3,1:T(8,128)S(1)} %select_bitcast_fusion.7), channel_id=1, source_target_pairs={{0,64},{4,68},{8,72},{12,76},{16,80},{20,84},{24,88},{28,92},{32,9... | collective-permute-start | bytes 393224 | tf_op jit(solution)/shard_map/ppermute | solution.py:25
  110.4 10.3 %collective-permute-start.20 = (f32[2,2,2,1,1,8,1152]{6,5,0,1,2,4,3:T(8,128)S(1)}, f32[2,2,2,1,1,8,1152]{6,5,0,1,2,4,3:T(8,128)S(1)}, u32[]{:S(2)}, u32[]{:S(2)}) collective-permute-start(f32[2,2,2,1,1,8,1152]{6,5,0,1,2,4,3:T(8,128)S(1)} %select_bitcast_fusion.4), channel_id=1, source_target_pairs={{0,32},{4,36},{8,40},{12,44},{16,48},{20,52},{24,56},{28,60},{32,0... | collective-permute-start | bytes 884744 | tf_op jit(solution)/shard_map/ppermute | solution.py:25
  117.2 5.9 %collective-permute-start.28 = (f32[2,1,1,1,1,8,1024]{6,5,4,3,2,1,0:T(8,128)S(1)}, f32[2,1,1,1,1,8,1024]{6,5,4,3,2,1,0:T(8,128)S(1)}, u32[]{:S(2)}, u32[]{:S(2)}) collective-permute-start(f32[2,1,1,1,1,8,1024]{6,5,4,3,2,1,0:T(8,128)S(1)} %select_bitcast_fusion.9), channel_id=1, source_target_pairs={{0,16},{4,20},{8,24},{12,28},{16,0},{20,4},{24,8},{28,12},{32,48},... | collective-permute-start | bytes 196616 | tf_op jit(solution)/shard_map/ppermute | solution.py:25
  120.7 6.7 %collective-permute-start.21 = (f32[2,2,1,1,1,8,1152]{6,5,0,1,4,3,2:T(8,128)S(1)}, f32[2,2,1,1,1,8,1152]{6,5,0,1,4,3,2:T(8,128)S(1)}, u32[]{:S(2)}, u32[]{:S(2)}) collective-permute-start(f32[2,2,1,1,1,8,1152]{6,5,0,1,4,3,2:T(8,128)S(1)} %select_bitcast_fusion.6), channel_id=1, source_target_pairs={{0,16},{4,20},{8,24},{12,28},{16,0},{20,4},{24,8},{28,12},{32,48},... | collective-permute-start | bytes 442376 | tf_op jit(solution)/shard_map/ppermute | solution.py:25
  127.5 6.4 %collective-permute-start.22 = (f32[2,1,1,1,1,8,1152]{6,5,4,3,2,1,0:T(8,128)S(1)}, f32[2,1,1,1,1,8,1152]{6,5,4,3,2,1,0:T(8,128)S(1)}, u32[]{:S(2)}, u32[]{:S(2)}) collective-permute-start(f32[2,1,1,1,1,8,1152]{6,5,4,3,2,1,0:T(8,128)S(1)} %select_bitcast_fusion.8), channel_id=1, source_target_pairs={{0,64},{4,68},{8,72},{12,76},{16,80},{20,84},{24,88},{28,92},{32,9... | collective-permute-start | bytes 221192 | tf_op jit(solution)/shard_map/ppermute | solution.py:25
  128.6 8.0 %collective-permute-start.29 = (f32[1,1,1,1,1,8,1024]{6,5,4,3,2,1,0:T(8,128)S(1)}, f32[1,1,1,1,1,8,1024]{6,5,4,3,2,1,0:T(8,128)S(1)}, u32[]{:S(2)}, u32[]{:S(2)}) collective-permute-start(f32[1,1,1,1,1,8,1024]{6,5,4,3,2,1,0:T(8,128)S(1)} %slice_select_fusion.1), channel_id=1, source_target_pairs={{0,128},{4,132},{8,136},{12,140},{16,144},{20,148},{24,152},{28,15... | collective-permute-start | bytes 98312 | tf_op jit(solution)/shard_map/ppermute | solution.py:25
  133.9 8.0 %collective-permute-start.23 = (f32[1,1,1,1,1,8,1152]{6,5,4,3,2,1,0:T(8,128)S(1)}, f32[1,1,1,1,1,8,1152]{6,5,4,3,2,1,0:T(8,128)S(1)}, u32[]{:S(2)}, u32[]{:S(2)}) collective-permute-start(f32[1,1,1,1,1,8,1152]{6,5,4,3,2,1,0:T(8,128)S(1)} %slice_select_fusion), channel_id=1, source_target_pairs={{0,128},{4,132},{8,136},{12,140},{16,144},{20,148},{24,152},{28,15... | collective-permute-start | bytes 110600 | tf_op jit(solution)/shard_map/ppermute | solution.py:25
  (22 other events, 136.1 us)
